TPU v7x, 512 devices: a whole 4x8x8 slice. The times are simulated.
512 devices in a mesh: row: 32 (over x, z), col: 16 (over y, core).
Axes of the slice: x: 4, y: 8, z: 8, core: 2. Of those that a mesh axis runs over, the one named last changes fastest.
Arguments:
- matrix: float32 [14336, 14336], P('row', 'col'), may hold values from -3 to 3
- reflectors: float32 [1, 64, 14336], P(None, None, 'row'), may hold values from -0.09375 to 0.09375
- factors: float32 [1, 64, 64], replicated, may hold values from -0.1 to 2, as said below
Outputs:
- updated: float32 [14336, 14336], P('row', 'col')
- companions: float32 [1, 64, 14336], P(None, None, 'row')
Inputs may be any that keep to these rules, and one draw needn't show every extreme that they name: `factors`: each factor is upper triangular (zero below the diagonal) with diagonal entries between 1 and 2.
All inputs are finite; a program needn't handle non-finite values.
Results may differ from a plain program's by a relative error of at most 0.0001.
Values sent between devices are 32-bit elements; how exact they have to be, the bound alone decides.
No kernel may reach another device: no remote copies, remote signals or barrier semaphores. Data moves between devices by JAX's collectives and lax.ppermute only.
A program may use at most 64 MiB of HBM per device.

v0:
```python
import jax
import jax.numpy as jnp
from jax import lax
from jax.sharding import PartitionSpec as P


def spread(block, axis, owner):
    block = jnp.where(lax.axis_index(axis) == owner, block, jnp.zeros_like(block))
    return lax.psum(block, axis)


def contract(left_side, right_side, left_dim, right_dim):
    return lax.dot_general(
        left_side,
        right_side,
        (((left_dim,), (right_dim,)), ((), ())),
        precision=lax.Precision.HIGHEST,
        preferred_element_type=jnp.float32,
    )


def reflector_blocks(values):
    group_ratio = lax.axis_size("row") // lax.axis_size("col")
    column = lax.axis_index("col")
    pieces = []
    for offset in range(group_ratio):
        root_index = column * group_ratio + offset
        pieces.append(spread(values, "row", root_index))
    return jnp.concatenate(pieces, axis=values.ndim - 1)


def shards(matrix, reflectors, factors):
    current = matrix
    reflector_cols = reflector_blocks(reflectors)
    v_rows = reflectors[0]
    v_cols = reflector_cols[0]
    factor = factors[0]
    partial_value = contract(v_cols, current, 1, 1)
    column_partial = contract(v_rows, current, 1, 0)
    row_sums = lax.psum(partial_value, "col")
    x_rows = contract(factor, row_sums, 0, 0)
    projected = lax.psum(contract(v_rows, x_rows, 1, 1), "row")
    mixing = contract(projected, factor, 0, 0)
    w_rows = x_rows - 0.5 * contract(mixing, v_rows, 1, 0)
    col_sums = lax.psum(column_partial, "row")
    x_cols = contract(factor, col_sums, 0, 0)
    w_cols = x_cols - 0.5 * contract(mixing, v_cols, 1, 0)
    current = current - contract(v_rows, w_cols, 0, 0) - contract(w_rows, v_cols, 0, 0)
    results = [w_rows]
    return (current, jnp.stack(results))


def solution(mesh):
    return jax.shard_map(
        shards,
        mesh=mesh,
        in_specs=(P("row", "col"), P(None, None, "row"), P()),
        out_specs=(P("row", "col"), P(None, None, "row")),
        check_vma=False,
    )
```

profile of v0, /device:TPU:32, one launch (start us, length us, event | category | flops | bytes accessed | tf_op | source)
XLA Modules:
  0.0 447.0 jit_solution(9648008019465141000)
XLA Ops:
  7.2 0.0 copy-start
  7.2 0.0 copy-start.2
  7.2 0.0 copy-start.1
  7.2 0.0 all-reduce.6.cloned.1.call-start
  7.3 3.3 fusion.7
  10.6 0.0 copy-done.2
  10.6 0.7 broadcast_select_fusion.1
  11.3 0.0 all-reduce.6.cloned.1.call-update
  11.3 0.0 all-reduce.4.cloned.1.call-start
  11.4 164.6 %all-reduce.6.cloned.1.call-done = (f32[1,64,448]{2,1,0:T(8,128)}, f32[1,64,448]{2,1,0:T(8,128)}, f32[64,896]{1,0:T(8,128)}) async-done(((f32[1,64,448]{2,1,0:T(8,128)}, f32[1,64,448]{2,1,0:T(8,128)}, f32[64,896]{1,0:T(8,128)}), (f32[1,64,448]{2,1,0:T(8,128)}, f32[1,64,448]{2,1,0:T(8,128)}, f32[64,896]{1,0:T(8,128)})) %all-reduce.6.cloned.1.call-update) | async-done | bytes 458768 | tf_op jit(solution)/shard_map/psum | solution.py:9
  175.9 0.0 copy-done.1
  176.0 3.3 fusion.9
  179.3 0.0 all-reduce.4.cloned.1.call-update
  179.3 109.2 %all-reduce.4.cloned.1.call-done = f32[64,448]{1,0:T(8,128)} async-done(((f32[64,448]{1,0:T(8,128)}), f32[64,448]{1,0:T(8,128)}) %all-reduce.4.cloned.1.call-update) | async-done | bytes 114704 | tf_op jit(solution)/shard_map/psum | solution.py:40
  288.5 1.2 fusion.12
  289.7 0.3 convolution_bitcast_fusion.1
  290.0 143.7 %psum.39 = f32[64,64]{0,1:T(8,128)S(1)} all-reduce(f32[64,64]{0,1:T(8,128)S(1)} %convolution_bitcast_fusion.1), channel_id=1, replica_groups=mesh['row'=32,'col'=16] {'row'}, use_global_device_ids=true, to_apply=%region_4.5 | all-reduce | flops 4096 | bytes 32768 | tf_op jit(solution)/shard_map/psum | solution.py:42
  433.7 0.2 fusion.10
  433.9 0.3 fusion.2
  434.2 0.0 copy-start.5
  434.2 1.0 convolution_multiply_fusion
  435.2 0.9 fusion.1
  436.1 1.5 fusion.4
  437.6 2.6 fusion
  (8 shorter events, 0.0 us)
Async XLA Ops:
  7.2 281.3 %copy-start = (f32[1,64,64]{2,1,0:T(8,128)S(1)}, f32[1,64,64]{2,1,0:T(8,128)}, u32[]{:S(2)}) copy-start(f32[1,64,64]{2,1,0:T(8,128)} %param.5) | copy-start | bytes 49156
  7.2 3.4 copy-start.2
  7.2 168.8 %copy-start.1 = (f32[448,896]{1,0:T(8,128)S(1)}, f32[448,896]{1,0:T(8,128)}, u32[]{:S(2)}) copy-start(f32[448,896]{1,0:T(8,128)} %param.3) | copy-start | bytes 4816900
  7.2 168.8 %all-reduce.6.cloned.1.call-start = ((), (), s32[]{:S(2)}) async-start(), calls=%async_computation.1 | async-start | bytes 983040 | tf_op jit(solution)/shard_map/psum | solution.py:9
  11.3 277.2 %all-reduce.4.cloned.1.call-start = ((), (), s32[]{:S(2)}) async-start(), calls=%async_computation | async-start | bytes 262144 | tf_op jit(solution)/shard_map/psum | solution.py:40
  176.0 258.2 %copy-start.3 = (f32[1,64,448]{2,1,0:T(8,128)S(1)}, f32[1,64,448]{2,1,0:T(8,128)}, u32[]{:S(2)}) copy-start(f32[1,64,448]{2,1,0:T(8,128)} %get-tuple-element.2) | copy-start | bytes 344068
  176.0 258.2 %copy-start.4 = (f32[1,64,448]{2,1,0:T(8,128)S(1)}, f32[1,64,448]{2,1,0:T(8,128)}, u32[]{:S(2)}) copy-start(f32[1,64,448]{2,1,0:T(8,128)} %get-tuple-element.3) | copy-start | bytes 344068
  176.0 259.2 %copy-start.6 = (f32[64,896]{1,0:T(8,128)S(1)}, f32[64,896]{1,0:T(8,128)}, u32[]{:S(2)}) copy-start(f32[64,896]{1,0:T(8,128)} %get-tuple-element.4) | copy-start | bytes 688132
  434.2 3.4 copy-start.5
Sparse Core Ops, SparseCore 0:
  12.3 163.6 all-reduce.5
  179.4 108.9 all-reduce.3
where the time goes:
time: 447 us
  waiting for transfers between devices  274 us (61%)
  blocking collectives  144 us (32%)
  matrix products  14.5 us (3%)
  between operations  14.2 us (3%)
    psum x1, waiting for transfers between devices, spread(): return lax.psum(block, axis)  165 us
    psum x1, blocking collectives, shards(): projected = lax.psum(contract(v_rows, x_rows, 1, 1), 'row')  144 us
    psum x1, waiting for transfers between devices, shards(): row_sums = lax.psum(partial_value, 'col')  109 us
    dot_general x10, matrix products, contract(): lax.dot_general(left_side, right_side, (((left_dim,), (right_dim,)), ((),...  14.5 us
  transfers between devices with their start and end apart: 2, of which 2 were waited for; matrix products, arithmetic and copies ran while one was open for 0% of the time, Pallas kernels for 0%

commit v1 on v0

v1 whole, which is shorter than its diff:
```python
import jax
import jax.numpy as jnp
from jax import lax
from jax.sharding import PartitionSpec as P


def contract(left_side, right_side, left_dim, right_dim):
    return lax.dot_general(
        left_side,
        right_side,
        (((left_dim,), (right_dim,)), ((), ())),
        precision=lax.Precision.HIGHEST,
        preferred_element_type=jnp.float32,
    )


def column_block_pairs(rows, cols, shift):
    group = rows // cols
    pairs = []
    for r in range(rows):
        for c in range(cols):
            target_row = group * c + (r % group - shift) % group
            pairs.append((r * cols + c, target_row * cols + r // group))
    return pairs


def to_column_blocks(values, rows, cols):
    group = rows // cols
    rounds = [
        lax.ppermute(values, ("row", "col"), column_block_pairs(rows, cols, shift))
        for shift in range(group)
    ]
    offset = lax.axis_index("row") % group
    blocks = []
    for part in range(group):
        block = rounds[0]
        for shift in range(1, group):
            block = jnp.where((part - offset) % group == shift, rounds[shift], block)
        blocks.append(block)
    return jnp.concatenate(blocks, axis=values.ndim - 1)


def make_shards(rows, cols):
    def shards(matrix, reflectors, factors):
        current = matrix
        v_rows = reflectors[0]
        factor = factors[0]
        v_cols = to_column_blocks(v_rows, rows, cols)
        partial_value = contract(v_cols, current, 1, 1)
        row_sums = jnp.sum(lax.all_gather(partial_value, "col"), axis=0)
        x_rows = contract(factor, row_sums, 0, 0)
        x_cols = to_column_blocks(x_rows, rows, cols)
        projected = jnp.sum(lax.all_gather(contract(v_rows, x_rows, 1, 1), "row"), axis=0)
        mixing = contract(projected, factor, 0, 0)
        w_rows = x_rows - 0.5 * contract(mixing, v_rows, 1, 0)
        w_cols = x_cols - 0.5 * contract(mixing, v_cols, 1, 0)
        current = current - contract(v_rows, w_cols, 0, 0) - contract(w_rows, v_cols, 0, 0)
        return (current, jnp.stack([w_rows]))

    return shards


def solution(mesh):
    return jax.shard_map(
        make_shards(mesh.shape["row"], mesh.shape["col"]),
        mesh=mesh,
        in_specs=(P("row", "col"), P(None, None, "row"), P()),
        out_specs=(P("row", "col"), P(None, None, "row")),
        check_vma=False,
    )
```

time: 447 us -> 233 us (0.52)
  waiting for transfers between devices: 274 us -> 88.6 us
  blocking collectives: 144 us -> 91.5 us
  starting transfers between devices: 0.08 us -> 27.1 us
  matrix products: 14.5 us -> 9.3 us
    psum x2 -> x0, waiting for transfers between devices: 274 us -> none  [the longest x1 165 us: spread(): return lax.psum(block, axis)]
    psum x1 -> x0, blocking collectives: 144 us -> none  [shards(): projected = lax.psum(contract(v_rows, x_rows, 1, 1), 'row')]
    all_gather x0 -> x1, blocking collectives: none -> 91.5 us  [shards(): lax.all_gather(contract(v_rows, x_rows, 1, 1), 'row')]
    all_gather x0 -> x1, waiting for transfers between devices: none -> 80.9 us  [shards(): row_sums = jnp.sum(lax.all_gather(partial_value, 'col'), axis=0)]
    ppermute x0 -> x4, starting transfers between devices: none -> 27 us  [to_column_blocks(): lax.ppermute(values, ('row', 'col'), column_block_pairs(rows, cols, shift))]
    ppermute x0 -> x4, waiting for transfers between devices: none -> 7.71 us  [to_column_blocks(): lax.ppermute(values, ('row', 'col'), column_block_pairs(rows, cols, shift))]
    dot_general x10 -> x8, matrix products: 14.5 us -> 9.3 us  [contract(): lax.dot_general(left_side, right_side, (((left_dim,), (right_dim,)), ((),...]
  transfers between devices with their start and end apart: 2 -> 5, of which waited for: 2 -> 2; matrix products, arithmetic and copies ran while one was open for 0% -> 0% of each run, Pallas kernels for 0% -> 0%
where the time goes in v1:
time: 233 us
  blocking collectives  91.5 us (39%)
  waiting for transfers between devices  88.6 us (38%)
  starting transfers between devices  27.1 us (12%)
  between operations  14.2 us (6%)
  matrix products  9.3 us (4%)
    all_gather x1, blocking collectives, shards(): lax.all_gather(contract(v_rows, x_rows, 1, 1), 'row')  91.5 us
    all_gather x1, waiting for transfers between devices, shards(): row_sums = jnp.sum(lax.all_gather(partial_value, 'col'), axis=0)  80.9 us
    ppermute x4, starting transfers between devices, to_column_blocks(): lax.ppermute(values, ('row', 'col'), column_block_pairs(rows, cols, shift))  27 us
    dot_general x8, matrix products, contract(): lax.dot_general(left_side, right_side, (((left_dim,), (right_dim,)), ((),...  9.3 us
    ppermute x4, waiting for transfers between devices, to_column_blocks(): lax.ppermute(values, ('row', 'col'), column_block_pairs(rows, cols, shift))  7.71 us
  transfers between devices with their start and end apart: 5, of which 2 were waited for; matrix products, arithmetic and copies ran while one was open for 0% of the time, Pallas kernels for 0%

profile of v1, /device:TPU:32, one launch (start us, length us, event | category | flops | bytes accessed | tf_op | source)
XLA Modules:
  0.0 232.8 jit_solution(7521428647609664123)
XLA Ops:
  7.2 0.0 copy-start
  7.2 0.0 all-gather.4.cloned.1.call-start
  7.2 4.5 %collective-permute-start.1 = (f32[64,448]{1,0:T(8,128)}, f32[64,448]{1,0:T(8,128)S(1)}, u32[]{:S(2)}, u32[]{:S(2)}) collective-permute-start(f32[64,448]{1,0:T(8,128)} %bitcast.32), channel_id=1, source_target_pairs={{0,0},{1,32},{2,64},{3,96},{4,128},{5,160},{6,192},{7,224},{8,256}... | collective-permute-start | bytes 344072 | tf_op jit(solution)/shard_map/ppermute | solution.py:30
  11.7 9.5 %collective-permute-start = (f32[64,448]{1,0:T(8,128)}, f32[64,448]{1,0:T(8,128)S(1)}, u32[]{:S(2)}, u32[]{:S(2)}) collective-permute-start(f32[64,448]{1,0:T(8,128)} %bitcast.33), channel_id=1, source_target_pairs={{0,16},{1,48},{2,80},{3,112},{4,144},{5,176},{6,208},{7,240},{8,27... | collective-permute-start | bytes 344072 | tf_op jit(solution)/shard_map/ppermute | solution.py:30
  21.3 7.7 %collective-permute-done = f32[64,448]{1,0:T(8,128)S(1)} collective-permute-done((f32[64,448]{1,0:T(8,128)}, f32[64,448]{1,0:T(8,128)S(1)}, u32[]{:S(2)}, u32[]{:S(2)}) %collective-permute-start) | collective-permute-done | bytes 114720 | tf_op jit(solution)/shard_map/ppermute | solution.py:30
  29.0 3.7 %fusion.5 = f32[64,448]{1,0:T(8,128)} fusion(f32[448,896]{1,0:T(8,128)} %param.3, f32[64,448]{1,0:T(8,128)S(1)} %get-tuple-element.5, f32[64,448]{1,0:T(8,128)S(1)} %get-tuple-element.4), kind=kOutput, calls=%fused_computation.11 | convolution fusion | flops 308338688 | bytes 1949696 | tf_op jit(solution)/shard_map/dot_general | solution.py:8
  32.7 0.0 all-gather.4.cloned.1.call-update
  32.7 80.9 %all-gather.4.cloned.1.call-done = f32[1024,448]{1,0:T(8,128)} async-done(((f32[64,448]{1,0:T(8,128)}), f32[1024,448]{1,0:T(8,128)}) %all-gather.4.cloned.1.call-update) | async-done | bytes 1835024 | tf_op jit(solution)/shard_map/all_gather | solution.py:50
  113.7 1.8 reduce_sum.18
  115.4 0.3 fusion.8
  115.8 0.3 convolution_bitcast_fusion
  116.0 7.1 %collective-permute-start.3 = (f32[64,448]{1,0:T(8,128)S(1)}, f32[64,448]{1,0:T(8,128)S(1)}, u32[]{:S(2)}, u32[]{:S(2)}) collective-permute-start(f32[64,448]{1,0:T(8,128)S(1)} %bitcast.34), channel_id=1, source_target_pairs={{0,0},{1,32},{2,64},{3,96},{4,128},{5,160},{6,192},{7,224},{8,256}... | collective-permute-start | bytes 344072 | tf_op jit(solution)/shard_map/ppermute | solution.py:30
  123.1 6.0 %collective-permute-start.2 = (f32[64,448]{1,0:T(8,128)S(1)}, f32[64,448]{1,0:T(8,128)S(1)}, u32[]{:S(2)}, u32[]{:S(2)}) collective-permute-start(f32[64,448]{1,0:T(8,128)S(1)} %bitcast.35), channel_id=1, source_target_pairs={{0,16},{1,48},{2,80},{3,112},{4,144},{5,176},{6,208},{7,240},{8,27... | collective-permute-start | bytes 344072 | tf_op jit(solution)/shard_map/ppermute | solution.py:30
  129.1 0.1 copy.5
  129.2 91.5 %all-gather.1 = f32[2048,64]{1,0:T(8,128)S(1)} all-gather(f32[64,64]{1,0:T(8,128)S(1)} %copy.5), channel_id=3, replica_groups=mesh['row'=32,'col'=16] {'row'}, dimensions={0}, use_global_device_ids=true | all-gather | bytes 540672 | tf_op jit(solution)/shard_map/all_gather | solution.py:53
  220.7 0.1 reduce_sum.19
  220.8 0.2 fusion.6
  221.0 0.3 fusion.1
  221.3 0.0 copy-start.3
  221.3 0.0 copy-start.1
  221.3 0.4 convolution_multiply_fusion
  221.7 0.0 collective-permute-done.2
  221.8 1.5 fusion.2
  223.3 2.6 %fusion = f32[448,896]{1,0:T(8,128)} fusion(f32[448,896]{1,0:T(8,128)S(1)} %copy-done.1, f32[896,448]{0,1:T(8,128)S(1)} %fusion.2, f32[64,448]{1,0:T(8,128)S(1)} %fusion.1, f32[64,448]{1,0:T(8,128)S(1)} %get-tuple-element.5, f32[64,448]{1,0:T(8,128)S(1)} %get-tuple-element.4), kind=kOutput, calls=%fused_computation.1 | convolution fusion | flops 309141504 | bytes 5160960 | tf_op jit(solution)/shard_map/dot_general | solution.py:8
  (9 shorter events, 0.1 us)
Async XLA Ops:
  7.2 108.3 %copy-start = (f32[1,64,64]{2,1,0:T(8,128)S(1)}, f32[1,64,64]{2,1,0:T(8,128)}, u32[]{:S(2)}) copy-start(f32[1,64,64]{2,1,0:T(8,128)} %param.5) | copy-start | bytes 49156
  7.2 106.5 %all-gather.4.cloned.1.call-start = ((), (), s32[]{:S(2)}) async-start(), calls=%async_computation | async-start | bytes 2228224 | tf_op jit(solution)/shard_map/all_gather | solution.py:50
  7.2 14.0 %collective-permute-start.1 = (f32[64,448]{1,0:T(8,128)}, f32[64,448]{1,0:T(8,128)S(1)}, u32[]{:S(2)}, u32[]{:S(2)}) collective-permute-start(f32[64,448]{1,0:T(8,128)} %bitcast.32), channel_id=1, source_target_pairs={{0,0},{1,32},{2,64},{3,96},{4,128},{5,160},{6,192},{7,224},{8,256}... | collective-permute-start | bytes 344072 | tf_op jit(solution)/shard_map/ppermute | solution.py:30
  11.7 17.3 %collective-permute-start = (f32[64,448]{1,0:T(8,128)}, f32[64,448]{1,0:T(8,128)S(1)}, u32[]{:S(2)}, u32[]{:S(2)}) collective-permute-start(f32[64,448]{1,0:T(8,128)} %bitcast.33), channel_id=1, source_target_pairs={{0,16},{1,48},{2,80},{3,112},{4,144},{5,176},{6,208},{7,240},{8,27... | collective-permute-start | bytes 344072 | tf_op jit(solution)/shard_map/ppermute | solution.py:30
  32.7 83.1 %copy-start.2 = (f32[1,64,448]{2,1,0:T(8,128)S(1)}, f32[1,64,448]{2,1,0:T(8,128)}, u32[]{:S(2)}) copy-start(f32[1,64,448]{2,1,0:T(8,128)} %param.4) | copy-start | bytes 344068
  116.0 105.7 %collective-permute-start.3 = (f32[64,448]{1,0:T(8,128)S(1)}, f32[64,448]{1,0:T(8,128)S(1)}, u32[]{:S(2)}, u32[]{:S(2)}) collective-permute-start(f32[64,448]{1,0:T(8,128)S(1)} %bitcast.34), channel_id=1, source_target_pairs={{0,0},{1,32},{2,64},{3,96},{4,128},{5,160},{6,192},{7,224},{8,256}... | collective-permute-start | bytes 344072 | tf_op jit(solution)/shard_map/ppermute | solution.py:30
  123.1 98.6 %collective-permute-start.2 = (f32[64,448]{1,0:T(8,128)S(1)}, f32[64,448]{1,0:T(8,128)S(1)}, u32[]{:S(2)}, u32[]{:S(2)}) collective-permute-start(f32[64,448]{1,0:T(8,128)S(1)} %bitcast.35), channel_id=1, source_target_pairs={{0,16},{1,48},{2,80},{3,112},{4,144},{5,176},{6,208},{7,240},{8,27... | collective-permute-start | bytes 344072 | tf_op jit(solution)/shard_map/ppermute | solution.py:30
  221.3 2.0 copy-start.3
  221.3 2.0 copy-start.1
Sparse Core Ops, SparseCore 0:
  32.9 80.7 all-gather.3

commit v2 on v1

v2 whole, which is shorter than its diff:
```python
import jax
import jax.numpy as jnp
from jax import lax
from jax.sharding import Mesh
from jax.sharding import PartitionSpec as P


def contract(left_side, right_side, left_dim, right_dim):
    return lax.dot_general(
        left_side,
        right_side,
        (((left_dim,), (right_dim,)), ((), ())),
        precision=lax.Precision.HIGHEST,
        preferred_element_type=jnp.float32,
    )


def gathered_sum(values, axes):
    for axis in axes:
        values = jnp.sum(lax.all_gather(values, axis), axis=0)
    return values


def column_block_pairs(rows, cols, shift):
    group = rows // cols
    pairs = []
    for r in range(rows):
        for c in range(cols):
            target_row = group * c + (r % group - shift) % group
            pairs.append((r * cols + c, target_row * cols + r // group))
    return pairs


def to_column_blocks(values, rows, cols, all_axes, row_index):
    group = rows // cols
    rounds = [
        lax.ppermute(values, all_axes, column_block_pairs(rows, cols, shift))
        for shift in range(group)
    ]
    offset = row_index % group
    blocks = []
    for part in range(group):
        block = rounds[0]
        for shift in range(1, group):
            block = jnp.where((part - offset) % group == shift, rounds[shift], block)
        blocks.append(block)
    return jnp.concatenate(blocks, axis=values.ndim - 1)


def make_shards(row_axes, col_axes, rows, cols):
    all_axes = tuple(row_axes) + tuple(col_axes)

    def shards(matrix, reflectors, factors):
        current = matrix
        v_rows = reflectors[0]
        factor = factors[0]
        row_index = lax.axis_index(tuple(row_axes))
        v_cols = to_column_blocks(v_rows, rows, cols, all_axes, row_index)
        col_sums = gathered_sum(contract(v_rows, current, 1, 0), row_axes[::-1])
        partial_value = contract(v_cols, current, 1, 1)
        partial_inner = contract(v_cols, col_sums, 1, 1)
        width = partial_value.shape[1]
        sums = gathered_sum(jnp.concatenate([partial_value, partial_inner], axis=1), col_axes[::-1])
        row_sums = sums[:, :width]
        inner = sums[:, width:]
        x_rows = contract(factor, row_sums, 0, 0)
        x_cols = contract(factor, col_sums, 0, 0)
        projected = contract(inner, factor, 0, 0)
        mixing = contract(projected, factor, 0, 0)
        w_rows = x_rows - 0.5 * contract(mixing, v_rows, 1, 0)
        w_cols = x_cols - 0.5 * contract(mixing, v_cols, 1, 0)
        current = current - contract(v_rows, w_cols, 0, 0) - contract(w_rows, v_cols, 0, 0)
        return (current, jnp.stack([w_rows]))

    return shards


def solution(mesh):
    row_axes, col_axes = ("x", "z"), ("y", "core")
    rows, cols = mesh.shape["row"], mesh.shape["col"]
    split = (4, rows // 4, cols // 2, 2) if rows % 4 == 0 and cols % 2 == 0 else None
    if split is None:
        row_axes, col_axes = ("row",), ("col",)
        fine = mesh
    else:
        fine = Mesh(mesh.devices.reshape(split), row_axes + col_axes)
    return jax.shard_map(
        make_shards(row_axes, col_axes, rows, cols),
        mesh=fine,
        in_specs=(P(row_axes, col_axes), P(None, None, row_axes), P()),
        out_specs=(P(row_axes, col_axes), P(None, None, row_axes)),
        check_vma=False,
    )
```

time: 233 us -> 174 us (0.75)
  the two profiles are of different devices: /device:TPU:32 before, /device:TPU:2 now
where the time goes in v2:
time: 174 us
  waiting for transfers between devices  82.6 us (47%)
  blocking collectives  51.4 us (30%)
  between operations  14.2 us (8%)
  matrix products  12.5 us (7%)
  starting transfers between devices  9.53 us (5%)
  other arithmetic  3.74 us (2%)
    all_gather x2, waiting for transfers between devices, gathered_sum(): values = jnp.sum(lax.all_gather(values, axis), axis=0)  54.1 us
    all_gather x2, blocking collectives, gathered_sum(): values = jnp.sum(lax.all_gather(values, axis), axis=0)  51.4 us
    ppermute x2, waiting for transfers between devices, to_column_blocks(): lax.ppermute(values, all_axes, column_block_pairs(rows, cols, shift))  28.5 us
    dot_general x11, matrix products, contract(): lax.dot_general(left_side, right_side, (((left_dim,), (right_dim,)), ((),...  12.5 us
    ppermute x2, starting transfers between devices, to_column_blocks(): lax.ppermute(values, all_axes, column_block_pairs(rows, cols, shift))  9.45 us
    reduce_sum x4, other arithmetic, gathered_sum(): values = jnp.sum(lax.all_gather(values, axis), axis=0)  3.64 us
  transfers between devices with their start and end apart: 4, of which 4 were waited for; matrix products, arithmetic and copies ran while one was open for 1% of the time, Pallas kernels for 0%

profile of v2, /device:TPU:2, one launch (start us, length us, event | category | flops | bytes accessed | tf_op | source)
XLA Modules:
  0.0 174.0 jit_solution(2003795575332353558)
XLA Ops:
  7.2 3.3 %fusion.20 = f32[64,896]{1,0:T(8,128)} fusion(f32[448,896]{1,0:T(8,128)} %param.3, f32[1,64,448]{2,1,0:T(8,128)} %param.4), kind=kOutput, calls=%fused_computation.29 | convolution fusion | flops 308281344 | bytes 1949696 | tf_op jit(solution)/shard_map/dot_general | solution.py:9
  10.7 6.3 %collective-permute-start = (f32[64,448]{1,0:T(8,128)S(1)}, f32[64,448]{1,0:T(8,128)S(1)}, u32[]{:S(2)}, u32[]{:S(2)}) collective-permute-start(f32[64,448]{1,0:T(8,128)S(1)} %bitcast.42), channel_id=1, source_target_pairs={{0,16},{1,48},{2,80},{3,112},{4,144},{5,176},{6,208},{7,240},{8,27... | collective-permute-start | bytes 344072 | tf_op jit(solution)/shard_map/ppermute | solution.py:37
  16.9 3.2 %collective-permute-start.1 = (f32[64,448]{1,0:T(8,128)S(1)}, f32[64,448]{1,0:T(8,128)S(1)}, u32[]{:S(2)}, u32[]{:S(2)}) collective-permute-start(f32[64,448]{1,0:T(8,128)S(1)} %bitcast.43), channel_id=1, source_target_pairs={{0,0},{1,32},{2,64},{3,96},{4,128},{5,160},{6,192},{7,224},{8,256}... | collective-permute-start | bytes 344072 | tf_op jit(solution)/shard_map/ppermute | solution.py:37
  20.2 0.1 collective-permute-done
  20.3 28.3 %collective-permute-done.1 = f32[64,448]{1,0:T(8,128)S(1)} collective-permute-done((f32[64,448]{1,0:T(8,128)S(1)}, f32[64,448]{1,0:T(8,128)S(1)}, u32[]{:S(2)}, u32[]{:S(2)}) %collective-permute-start.1) | collective-permute-done | bytes 114720 | tf_op jit(solution)/shard_map/ppermute | solution.py:37
  48.7 1.7 fusion.5
  50.3 9.0 %all-gather.7.cloned.1.call-done = f32[512,896]{1,0:T(8,128)} async-done(((f32[64,896]{1,0:T(8,128)}), f32[512,896]{1,0:T(8,128)}) %all-gather.7.cloned.1.call-update) | async-done | bytes 1835024 | tf_op jit(solution)/shard_map/all_gather | solution.py:20
  59.3 1.6 reduce_sum.36
  60.9 49.4 %all-gather.1 = f32[256,896]{1,0:T(8,128)S(1)} all-gather(f32[64,896]{1,0:T(8,128)S(1)} %reduce_sum.36), channel_id=3, replica_groups=mesh['x'=4,'z'=8,'y'=8,'core'=2] {'x'}, dimensions={0}, use_global_device_ids=true | all-gather | bytes 1146880 | tf_op jit(solution)/shard_map/all_gather | solution.py:20
  110.3 0.1 reduce_sum.37
  110.4 0.4 fusion.4
  110.8 0.1 pad_maximum_fusion.1
  110.9 2.0 %all-gather.2 = f32[128,512]{1,0:T(8,128)S(1)} all-gather(f32[64,512]{1,0:T(8,128)S(1)} %pad_maximum_fusion.1), channel_id=4, replica_groups=mesh['x'=4,'z'=8,'y'=8,'core'=2] {'core'}, dimensions={0}, use_global_device_ids=true | all-gather | bytes 393216 | tf_op jit(solution)/shard_map/all_gather | solution.py:20
  112.9 0.7 reduce_sum.38
  113.6 0.9 convolution_bitcast_fusion
  114.5 45.1 %all-gather.9.cloned.1.call-done = f32[512,512]{1,0:T(8,128)} async-done(((f32[64,512]{1,0:T(8,128)}), f32[512,512]{1,0:T(8,128)}) %all-gather.9.cloned.1.call-update) | async-done | bytes 1048592 | tf_op jit(solution)/shard_map/all_gather | solution.py:20
  159.6 1.3 reduce_sum.39
  160.9 0.3 fusion.6
  161.2 0.2 fusion.9
  161.5 0.3 convolution_multiply_fusion.1
  161.8 0.3 fusion.2
  162.1 1.0 fusion.1
  163.1 1.5 fusion.18
  164.6 2.6 %fusion = f32[448,896]{1,0:T(8,128)} fusion(f32[448,896]{1,0:T(8,128)S(1)} %copy-done.1, f32[896,448]{0,1:T(8,128)S(1)} %fusion.18, f32[64,448]{1,0:T(8,128)S(1)} %fusion.2, f32[64,448]{1,0:T(8,128)S(1)} %get-tuple-element.3, f32[64,448]{1,0:T(8,128)S(1)} %get-tuple-element.2), kind=kOutput, calls=%fused_computation.1 | convolution fusion | flops 309141504 | bytes 5160960 | tf_op jit(solution)/shard_map/dot_general | solution.py:9
  (13 shorter events, 0.2 us)
Async XLA Ops:
  7.2 106.4 %copy-start = (f32[1,64,64]{2,1,0:T(8,128)S(1)}, f32[1,64,64]{2,1,0:T(8,128)}, u32[]{:S(2)}) copy-start(f32[1,64,64]{2,1,0:T(8,128)} %param.5) | copy-start | bytes 49156
  7.2 3.5 %copy-start.2 = (f32[1,64,448]{2,1,0:T(8,128)S(1)}, f32[1,64,448]{2,1,0:T(8,128)}, u32[]{:S(2)}) copy-start(f32[1,64,448]{2,1,0:T(8,128)} %param.4) | copy-start | bytes 344068
  7.2 41.5 %copy-start.1 = (f32[448,896]{1,0:T(8,128)S(1)}, f32[448,896]{1,0:T(8,128)}, u32[]{:S(2)}) copy-start(f32[448,896]{1,0:T(8,128)} %param.3) | copy-start | bytes 4816900
  7.2 52.1 %all-gather.7.cloned.1.call-start = ((), (), s32[]{:S(2)}) async-start(), calls=%async_computation | async-start | bytes 2064384 | tf_op jit(solution)/shard_map/all_gather | solution.py:20
  10.6 149.0 %all-gather.9.cloned.1.call-start = ((), (), s32[]{:S(2)}) async-start(), calls=%async_computation.1 | async-start | bytes 1179648 | tf_op jit(solution)/shard_map/all_gather | solution.py:20
  10.7 9.6 %collective-permute-start = (f32[64,448]{1,0:T(8,128)S(1)}, f32[64,448]{1,0:T(8,128)S(1)}, u32[]{:S(2)}, u32[]{:S(2)}) collective-permute-start(f32[64,448]{1,0:T(8,128)S(1)} %bitcast.42), channel_id=1, source_target_pairs={{0,16},{1,48},{2,80},{3,112},{4,144},{5,176},{6,208},{7,240},{8,27... | collective-permute-start | bytes 344072 | tf_op jit(solution)/shard_map/ppermute | solution.py:37
  16.9 31.7 %collective-permute-start.1 = (f32[64,448]{1,0:T(8,128)S(1)}, f32[64,448]{1,0:T(8,128)S(1)}, u32[]{:S(2)}, u32[]{:S(2)}) collective-permute-start(f32[64,448]{1,0:T(8,128)S(1)} %bitcast.43), channel_id=1, source_target_pairs={{0,0},{1,32},{2,64},{3,96},{4,128},{5,160},{6,192},{7,224},{8,256}... | collective-permute-start | bytes 344072 | tf_op jit(solution)/shard_map/ppermute | solution.py:37
  162.1 2.5 %copy-start.3 = (f32[64,448]{1,0:T(8,128)}, f32[64,448]{1,0:T(8,128)S(1)}, u32[]{:S(2)}) copy-start(f32[64,448]{1,0:T(8,128)S(1)} %fusion.2) | copy-start | bytes 344068
Sparse Core Ops, SparseCore 0:
  10.7 48.5 all-gather.6
  113.7 45.8 all-gather.8

commit v3 on v2

--- a/solution.py
+++ b/solution.py
@@ -19,6 +19,27 @@
     for axis in axes:
         values = jnp.sum(lax.all_gather(values, axis), axis=0)
     return values
+
+
+def split_sum(values, axis, split_axis):
+    width = values.shape[1] // 2
+    mine = jnp.where(lax.axis_index(split_axis) == 0, values[:, :width], values[:, width:])
+    total = gathered_sum(mine, (axis,))
+    both = lax.all_gather(total, split_axis)
+    return jnp.concatenate([both[0], both[1]], axis=1)
+
+
+def scattered_sum(values, axis, parts):
+    chunks = values.reshape((parts, values.shape[0] // parts) + values.shape[1:])
+    mine = jnp.sum(lax.all_to_all(chunks, axis, 0, 0, tiled=False), axis=0)
+    return lax.all_gather(mine, axis, tiled=True)
+
+
+def halves_sum(values, axis):
+    width = values.shape[1] // 2
+    left = gathered_sum(values[:, :width], (axis,))
+    right = gathered_sum(values[:, width:], (axis,))
+    return jnp.concatenate([left, right], axis=1)
 
 
 def column_block_pairs(rows, cols, shift):
@@ -56,11 +77,11 @@
         factor = factors[0]
         row_index = lax.axis_index(tuple(row_axes))
         v_cols = to_column_blocks(v_rows, rows, cols, all_axes, row_index)
-        col_sums = gathered_sum(contract(v_rows, current, 1, 0), row_axes[::-1])
+        col_sums = scattered_sum(gathered_sum(contract(v_rows, current, 1, 0), row_axes[:1]), row_axes[1], lax.axis_size(row_axes[1]))
         partial_value = contract(v_cols, current, 1, 1)
         partial_inner = contract(v_cols, col_sums, 1, 1)
         width = partial_value.shape[1]
-        sums = gathered_sum(jnp.concatenate([partial_value, partial_inner], axis=1), col_axes[::-1])
+        sums = split_sum(gathered_sum(jnp.concatenate([partial_value, partial_inner], axis=1), col_axes[1:]), col_axes[0], col_axes[1])
         row_sums = sums[:, :width]
         inner = sums[:, width:]
         x_rows = contract(factor, row_sums, 0, 0)

time: 174 us -> 137 us (0.79)
  the two profiles are of different devices: /device:TPU:2 before, /device:TPU:21 now
where the time goes in v3:
time: 137 us
  blocking collectives  83.6 us (61%)
  starting transfers between devices  25.3 us (18%)
  waiting for transfers between devices  14.4 us (11%)
  matrix products  11.7 us (9%)
    all_gather x3, blocking collectives, gathered_sum(): values = jnp.sum(lax.all_gather(values, axis), axis=0)  56.9 us
    all_gather x1, blocking collectives, scattered_sum(): return lax.all_gather(mine, axis, tiled=True)  18.6 us
    ppermute x2, waiting for transfers between devices, to_column_blocks(): lax.ppermute(values, all_axes, column_block_pairs(rows, cols, shift))  14.4 us
    ppermute x2, starting transfers between devices, to_column_blocks(): lax.ppermute(values, all_axes, column_block_pairs(rows, cols, shift))  13.3 us
    all_to_all x1, starting transfers between devices, scattered_sum(): mine = jnp.sum(lax.all_to_all(chunks, axis, 0, 0, tiled=False), axis=0)  12 us
    dot_general x11, matrix products, contract(): lax.dot_general(left_side, right_side, (((left_dim,), (right_dim,)), ((),...  11.7 us
    all_gather x1, blocking collectives, split_sum(): both = lax.all_gather(total, split_axis)  8.06 us
  transfers between devices with their start and end apart: 3, of which 2 were waited for; matrix products, arithmetic and copies ran while one was open for 4% of the time, Pallas kernels for 0%

profile of v3, /device:TPU:21, one launch (start us, length us, event | category | flops | bytes accessed | tf_op | source)
XLA Modules:
  0.0 136.7 jit_solution(6682446254072141484)
XLA Ops:
  0.6 0.0 copy-start
  0.6 11.4 %collective-permute-start = (f32[64,448]{1,0:T(8,128)}, f32[64,448]{1,0:T(8,128)S(1)}, u32[]{:S(2)}, u32[]{:S(2)}) collective-permute-start(f32[64,448]{1,0:T(8,128)} %bitcast.42), channel_id=1, source_target_pairs={{0,16},{1,48},{2,80},{3,112},{4,144},{5,176},{6,208},{7,240},{8,27... | collective-permute-start | bytes 344072 | tf_op jit(solution)/shard_map/ppermute | solution.py:58
  12.0 1.9 %collective-permute-start.1 = (f32[64,448]{1,0:T(8,128)}, f32[64,448]{1,0:T(8,128)S(1)}, u32[]{:S(2)}, u32[]{:S(2)}) collective-permute-start(f32[64,448]{1,0:T(8,128)} %bitcast.43), channel_id=1, source_target_pairs={{0,0},{1,32},{2,64},{3,96},{4,128},{5,160},{6,192},{7,224},{8,256}... | collective-permute-start | bytes 344072 | tf_op jit(solution)/shard_map/ppermute | solution.py:58
  14.0 2.5 %fusion.21 = f32[64,896]{1,0:T(8,128)S(1)} fusion(f32[448,896]{1,0:T(8,128)} %param.3, f32[1,64,448]{2,1,0:T(8,128)} %param.4), kind=kOutput, calls=%fused_computation.32 | convolution fusion | flops 308281344 | bytes 1949696 | tf_op jit(solution)/shard_map/dot_general | solution.py:9
  16.5 13.0 %all-gather = f32[256,896]{1,0:T(8,128)S(1)} all-gather(f32[64,896]{1,0:T(8,128)S(1)} %fusion.21), channel_id=2, replica_groups=mesh['x'=4,'z'=8,'y'=8,'core'=2] {'x'}, dimensions={0}, use_global_device_ids=true | all-gather | bytes 1146880 | tf_op jit(solution)/shard_map/all_gather | solution.py:20
  29.5 0.7 reduce_sum.36
  30.2 12.0 %all-to-all-start = ((f32[8,8,896]{2,1,0:T(8,128)}), f32[8,8,896]{2,1,0:T(8,128)S(1)}, u32[]{:S(2)}, u32[]{:S(2)}) async-start(f32[8,8,896]{2,1,0:T(8,128)} %bitcast.2), calls=%async_computation | async-start | bytes 458752 | tf_op jit(solution)/shard_map/all_to_all | solution.py:34
  42.3 11.1 %collective-permute-done = f32[64,448]{1,0:T(8,128)S(1)} collective-permute-done((f32[64,448]{1,0:T(8,128)}, f32[64,448]{1,0:T(8,128)S(1)}, u32[]{:S(2)}, u32[]{:S(2)}) %collective-permute-start) | collective-permute-done | bytes 114720 | tf_op jit(solution)/shard_map/ppermute | solution.py:58
  53.3 3.3 %collective-permute-done.1 = f32[64,448]{1,0:T(8,128)S(1)} collective-permute-done((f32[64,448]{1,0:T(8,128)}, f32[64,448]{1,0:T(8,128)S(1)}, u32[]{:S(2)}, u32[]{:S(2)}) %collective-permute-start.1) | collective-permute-done | bytes 114720 | tf_op jit(solution)/shard_map/ppermute | solution.py:58
  56.7 1.7 %fusion.5 = f32[64,448]{1,0:T(8,128)S(1)} fusion(f32[448,896]{1,0:T(8,128)S(1)} %copy-done.1, f32[64,448]{1,0:T(8,128)S(1)} %get-tuple-element.3, f32[64,448]{1,0:T(8,128)S(1)} %get-tuple-element.2), kind=kOutput, calls=%fused_computation.16 | convolution fusion | flops 308338688 | bytes 1949696 | tf_op jit(solution)/shard_map/dot_general | solution.py:9
  58.3 18.6 %all_gather.29 = f32[64,896]{1,0:T(8,128)S(1)} all-gather(f32[8,896]{1,0:T(8,128)S(1)} %reduce_sum.37), channel_id=1, replica_groups=mesh['x'=4,'z'=8,'y'=8,'core'=2] {'z'}, dimensions={0}, use_global_device_ids=true | all-gather | bytes 258048 | tf_op jit(solution)/shard_map/all_gather | solution.py:35
  76.9 0.4 fusion.4
  77.3 0.1 pad_maximum_fusion.3
  77.4 5.2 %all-gather.1 = f32[128,512]{1,0:T(8,128)S(1)} all-gather(f32[64,512]{1,0:T(8,128)S(1)} %pad_maximum_fusion.3), channel_id=3, replica_groups=mesh['x'=4,'z'=8,'y'=8,'core'=2] {'core'}, dimensions={0}, use_global_device_ids=true | all-gather | bytes 393216 | tf_op jit(solution)/shard_map/all_gather | solution.py:20
  82.7 0.9 convolution_bitcast_fusion
  83.6 38.7 %all-gather.2 = f32[512,256]{1,0:T(8,128)S(1)} all-gather(f32[64,256]{1,0:T(8,128)S(1)} %slice_select_fusion), channel_id=4, replica_groups=mesh['x'=4,'z'=8,'y'=8,'core'=2] {'y'}, dimensions={0}, use_global_device_ids=true | all-gather | bytes 589824 | tf_op jit(solution)/shard_map/all_gather | solution.py:20
  122.4 8.1 %all-gather.3 = f32[128,256]{1,0:T(8,128)S(1)} all-gather(f32[64,256]{1,0:T(8,128)S(1)} %reduce_sum.39), channel_id=5, replica_groups=mesh['x'=4,'z'=8,'y'=8,'core'=2] {'core'}, dimensions={0}, use_global_device_ids=true | all-gather | bytes 196608 | tf_op jit(solution)/shard_map/all_gather | solution.py:28
  130.4 0.3 fusion.6
  130.8 0.2 fusion.9
  131.0 0.3 convolution_multiply_fusion.1
  131.3 1.0 fusion.1
  132.3 1.5 %fusion.19 = f32[896,448]{0,1:T(8,128)S(1)} fusion(f32[64,896]{0,1:T(8,128)S(1)} %fusion.1, f32[1,64,448]{2,1,0:T(8,128)S(1)} %copy-done.2), kind=kOutput, calls=%fused_computation.30 | convolution fusion | flops 308281344 | bytes 1949696 | tf_op jit(solution)/shard_map/dot_general | solution.py:9
  133.7 0.3 fusion.2
  134.1 2.6 %fusion = f32[448,896]{1,0:T(8,128)} fusion(f32[448,896]{1,0:T(8,128)S(1)} %copy-done.1, f32[896,448]{0,1:T(8,128)S(1)} %fusion.19, f32[64,448]{1,0:T(8,128)S(1)} %fusion.2, f32[64,448]{1,0:T(8,128)S(1)} %get-tuple-element.3, f32[64,448]{1,0:T(8,128)S(1)} %get-tuple-element.2), kind=kOutput, calls=%fused_computation.1 | convolution fusion | flops 309141504 | bytes 5160960 | tf_op jit(solution)/shard_map/dot_general | solution.py:9
  (14 shorter events, 0.1 us)
Async XLA Ops:
  0.6 82.1 %copy-start = (f32[1,64,64]{2,1,0:T(8,128)S(1)}, f32[1,64,64]{2,1,0:T(8,128)}, u32[]{:S(2)}) copy-start(f32[1,64,64]{2,1,0:T(8,128)} %param.5) | copy-start | bytes 49156
  0.6 52.7 %collective-permute-start = (f32[64,448]{1,0:T(8,128)}, f32[64,448]{1,0:T(8,128)S(1)}, u32[]{:S(2)}, u32[]{:S(2)}) collective-permute-start(f32[64,448]{1,0:T(8,128)} %bitcast.42), channel_id=1, source_target_pairs={{0,16},{1,48},{2,80},{3,112},{4,144},{5,176},{6,208},{7,240},{8,27... | collective-permute-start | bytes 344072 | tf_op jit(solution)/shard_map/ppermute | solution.py:58
  12.0 44.6 %collective-permute-start.1 = (f32[64,448]{1,0:T(8,128)}, f32[64,448]{1,0:T(8,128)S(1)}, u32[]{:S(2)}, u32[]{:S(2)}) collective-permute-start(f32[64,448]{1,0:T(8,128)} %bitcast.43), channel_id=1, source_target_pairs={{0,0},{1,32},{2,64},{3,96},{4,128},{5,160},{6,192},{7,224},{8,256}... | collective-permute-start | bytes 344072 | tf_op jit(solution)/shard_map/ppermute | solution.py:58
  16.5 40.1 %copy-start.1 = (f32[448,896]{1,0:T(8,128)S(1)}, f32[448,896]{1,0:T(8,128)}, u32[]{:S(2)}) copy-start(f32[448,896]{1,0:T(8,128)} %param.3) | copy-start | bytes 4816900
  30.2 28.1 %all-to-all-start = ((f32[8,8,896]{2,1,0:T(8,128)}), f32[8,8,896]{2,1,0:T(8,128)S(1)}, u32[]{:S(2)}, u32[]{:S(2)}) async-start(f32[8,8,896]{2,1,0:T(8,128)} %bitcast.2), calls=%async_computation | async-start | bytes 458752 | tf_op jit(solution)/shard_map/all_to_all | solution.py:34
  82.7 48.3 %copy-start.2 = (f32[1,64,448]{2,1,0:T(8,128)S(1)}, f32[1,64,448]{2,1,0:T(8,128)}, u32[]{:S(2)}) copy-start(f32[1,64,448]{2,1,0:T(8,128)} %param.4) | copy-start | bytes 344068
  134.1 2.7 %copy-start.3 = (f32[64,448]{1,0:T(8,128)}, f32[64,448]{1,0:T(8,128)S(1)}, u32[]{:S(2)}) copy-start(f32[64,448]{1,0:T(8,128)S(1)} %fusion.2) | copy-start | bytes 344068

commit v4 on v3

--- a/solution.py
+++ b/solution.py
@@ -52,12 +52,39 @@
     return pairs
 
 
+def staged_route(rows, cols):
+    sizes = (4, rows // 4, cols // 2, 2)
+    if rows % 4 or cols % 2 or sizes[2] % sizes[0]:
+        return None
+    k = sizes[2] // sizes[0]
+
+    def split(i):
+        return (i // (sizes[1] * sizes[2] * 2), (i // (sizes[2] * 2)) % sizes[1], (i // 2) % sizes[2], i % 2)
+
+    def join(x, z, y, core):
+        return ((x * sizes[1] + z) * sizes[2] + y) * 2 + core
+
+    def hop(i):
+        x, z, y, core = split(i)
+        return join(y // k, z, k * x + y % k, core)
+
+    return [(i, hop(i)) for i in range(rows * cols)]
+
+
 def to_column_blocks(values, rows, cols, all_axes, row_index):
     group = rows // cols
-    rounds = [
-        lax.ppermute(values, all_axes, column_block_pairs(rows, cols, shift))
-        for shift in range(group)
-    ]
+    first = staged_route(rows, cols)
+    if first is None:
+        rounds = [
+            lax.ppermute(values, all_axes, column_block_pairs(rows, cols, shift))
+            for shift in range(group)
+        ]
+    else:
+        moved = lax.ppermute(values, all_axes, first)
+        rounds = []
+        for shift in range(group):
+            final = dict(column_block_pairs(rows, cols, shift))
+            rounds.append(lax.ppermute(moved, all_axes, [(mid, final[i]) for i, mid in first]))
     offset = row_index % group
     blocks = []
     for part in range(group):

time: 137 us -> 129 us (0.942)
  the two profiles are of different devices: /device:TPU:21 before, /device:TPU:1 now
where the time goes in v4:
time: 129 us; the launch traced here: 128 us
  blocking collectives  84.7 us (66%)
  starting transfers between devices  22.7 us (18%)
  matrix products  11.7 us (9%)
  waiting for transfers between devices  7.28 us (6%)
    all_gather x3, blocking collectives, gathered_sum(): values = jnp.sum(lax.all_gather(values, axis), axis=0)  57.7 us
    all_gather x1, blocking collectives, scattered_sum(): return lax.all_gather(mine, axis, tiled=True)  18.9 us
    dot_general x11, matrix products, contract(): lax.dot_general(left_side, right_side, (((left_dim,), (right_dim,)), ((),...  11.7 us
    ppermute x2, starting transfers between devices, to_column_blocks(): lax.ppermute(moved, all_axes, [(mid, final[i]) for i, mid in first])  11.1 us
    all_to_all x1, starting transfers between devices, scattered_sum(): mine = jnp.sum(lax.all_to_all(chunks, axis, 0, 0, tiled=False), axis=0)  10.1 us
    all_gather x1, blocking collectives, split_sum(): both = lax.all_gather(total, split_axis)  8.06 us
    all_to_all x1, waiting for transfers between devices, scattered_sum(): mine = jnp.sum(lax.all_to_all(chunks, axis, 0, 0, tiled=False), axis=0)  7.27 us
  transfers between devices with their start and end apart: 4, of which 1 were waited for; matrix products, arithmetic and copies ran while one was open for 4% of the time, Pallas kernels for 0%

profile of v4, /device:TPU:1, one launch (start us, length us, event | category | flops | bytes accessed | tf_op | source)
XLA Modules:
  0.0 128.1 jit_solution(3366607977221600493)
XLA Ops:
  0.6 0.0 copy-start
  0.6 1.6 %collective-permute-start = (f32[64,448]{1,0:T(8,128)}, f32[64,448]{1,0:T(8,128)S(1)}, u32[]{:S(2)}, u32[]{:S(2)}) collective-permute-start(f32[64,448]{1,0:T(8,128)} %bitcast.42), channel_id=1, source_target_pairs={{0,0},{1,1},{2,2},{3,3},{4,128},{5,129},{6,130},{7,131},{8,256},{9... | collective-permute-start | bytes 344072 | tf_op jit(solution)/shard_map/ppermute | solution.py:83
  2.2 2.5 %fusion.21 = f32[64,896]{1,0:T(8,128)S(1)} fusion(f32[448,896]{1,0:T(8,128)} %param.3, f32[1,64,448]{2,1,0:T(8,128)} %param.4), kind=kOutput, calls=%fused_computation.32 | convolution fusion | flops 308281344 | bytes 1949696 | tf_op jit(solution)/shard_map/dot_general | solution.py:9
  4.8 7.3 %collective-permute-start.2 = (f32[64,448]{1,0:T(8,128)S(1)}, f32[64,448]{1,0:T(8,128)S(1)}, u32[]{:S(2)}, u32[]{:S(2)}) collective-permute-start(f32[64,448]{1,0:T(8,128)S(1)} %collective-permute-done), channel_id=1, source_target_pairs={{0,0},{1,32},{2,64},{3,96},{128,128},{129,160},{130,192},{131,224}... | collective-permute-start | bytes 344072 | tf_op jit(solution)/shard_map/ppermute | solution.py:87
  12.1 3.7 %collective-permute-start.1 = (f32[64,448]{1,0:T(8,128)S(1)}, f32[64,448]{1,0:T(8,128)S(1)}, u32[]{:S(2)}, u32[]{:S(2)}) collective-permute-start(f32[64,448]{1,0:T(8,128)S(1)} %collective-permute-done), channel_id=1, source_target_pairs={{0,16},{1,48},{2,80},{3,112},{128,144},{129,176},{130,208},{131,24... | collective-permute-start | bytes 344072 | tf_op jit(solution)/shard_map/ppermute | solution.py:87
  15.8 23.0 %all-gather = f32[256,896]{1,0:T(8,128)S(1)} all-gather(f32[64,896]{1,0:T(8,128)S(1)} %fusion.21), channel_id=2, replica_groups=mesh['x'=4,'z'=8,'y'=8,'core'=2] {'x'}, dimensions={0}, use_global_device_ids=true | all-gather | bytes 1146880 | tf_op jit(solution)/shard_map/all_gather | solution.py:20
  38.9 0.7 reduce_sum.36
  39.6 10.1 %all-to-all-start = ((f32[8,8,896]{2,1,0:T(8,128)}), f32[8,8,896]{2,1,0:T(8,128)S(1)}, u32[]{:S(2)}, u32[]{:S(2)}) async-start(f32[8,8,896]{2,1,0:T(8,128)} %bitcast.2), calls=%async_computation | async-start | bytes 458752 | tf_op jit(solution)/shard_map/all_to_all | solution.py:34
  49.8 1.7 %fusion.5 = f32[64,448]{1,0:T(8,128)S(1)} fusion(f32[448,896]{1,0:T(8,128)S(1)} %copy-done.1, f32[64,448]{1,0:T(8,128)S(1)} %get-tuple-element.3, f32[64,448]{1,0:T(8,128)S(1)} %get-tuple-element.2), kind=kOutput, calls=%fused_computation.16 | convolution fusion | flops 308338688 | bytes 1949696 | tf_op jit(solution)/shard_map/dot_general | solution.py:9
  51.4 7.3 %all-to-all-done = f32[8,8,896]{2,1,0:T(8,128)S(1)} async-done(((f32[8,8,896]{2,1,0:T(8,128)}), f32[8,8,896]{2,1,0:T(8,128)S(1)}, u32[]{:S(2)}, u32[]{:S(2)}) %all-to-all-start) | async-done | bytes 229408 | tf_op jit(solution)/shard_map/all_to_all | solution.py:34
  58.7 18.9 %all_gather.29 = f32[64,896]{1,0:T(8,128)S(1)} all-gather(f32[8,896]{1,0:T(8,128)S(1)} %reduce_sum.37), channel_id=1, replica_groups=mesh['x'=4,'z'=8,'y'=8,'core'=2] {'z'}, dimensions={0}, use_global_device_ids=true | all-gather | bytes 258048 | tf_op jit(solution)/shard_map/all_gather | solution.py:35
  77.7 0.4 fusion.4
  78.1 0.1 pad_maximum_fusion.3
  78.2 12.4 %all-gather.1 = f32[128,512]{1,0:T(8,128)S(1)} all-gather(f32[64,512]{1,0:T(8,128)S(1)} %pad_maximum_fusion.3), channel_id=3, replica_groups=mesh['x'=4,'z'=8,'y'=8,'core'=2] {'core'}, dimensions={0}, use_global_device_ids=true | all-gather | bytes 393216 | tf_op jit(solution)/shard_map/all_gather | solution.py:20
  90.6 0.9 convolution_bitcast_fusion
  91.5 22.2 %all-gather.2 = f32[512,256]{1,0:T(8,128)S(1)} all-gather(f32[64,256]{1,0:T(8,128)S(1)} %slice_select_fusion), channel_id=4, replica_groups=mesh['x'=4,'z'=8,'y'=8,'core'=2] {'y'}, dimensions={0}, use_global_device_ids=true | all-gather | bytes 589824 | tf_op jit(solution)/shard_map/all_gather | solution.py:20
  113.8 8.1 %all-gather.3 = f32[128,256]{1,0:T(8,128)S(1)} all-gather(f32[64,256]{1,0:T(8,128)S(1)} %reduce_sum.39), channel_id=5, replica_groups=mesh['x'=4,'z'=8,'y'=8,'core'=2] {'core'}, dimensions={0}, use_global_device_ids=true | all-gather | bytes 196608 | tf_op jit(solution)/shard_map/all_gather | solution.py:28
  121.8 0.3 fusion.6
  122.2 0.2 fusion.9
  122.4 0.3 convolution_multiply_fusion.1
  122.7 1.0 fusion.1
  123.7 1.5 %fusion.19 = f32[896,448]{0,1:T(8,128)S(1)} fusion(f32[64,896]{0,1:T(8,128)S(1)} %fusion.1, f32[1,64,448]{2,1,0:T(8,128)S(1)} %copy-done.2), kind=kOutput, calls=%fused_computation.30 | convolution fusion | flops 308281344 | bytes 1949696 | tf_op jit(solution)/shard_map/dot_general | solution.py:9
  125.1 0.3 fusion.2
  125.5 2.6 %fusion = f32[448,896]{1,0:T(8,128)} fusion(f32[448,896]{1,0:T(8,128)S(1)} %copy-done.1, f32[896,448]{0,1:T(8,128)S(1)} %fusion.19, f32[64,448]{1,0:T(8,128)S(1)} %fusion.2, f32[64,448]{1,0:T(8,128)S(1)} %get-tuple-element.3, f32[64,448]{1,0:T(8,128)S(1)} %get-tuple-element.2), kind=kOutput, calls=%fused_computation.1 | convolution fusion | flops 309141504 | bytes 5160960 | tf_op jit(solution)/shard_map/dot_general | solution.py:9
  (16 shorter events, 0.1 us)
Async XLA Ops:
  0.6 90.0 %copy-start = (f32[1,64,64]{2,1,0:T(8,128)S(1)}, f32[1,64,64]{2,1,0:T(8,128)}, u32[]{:S(2)}) copy-start(f32[1,64,64]{2,1,0:T(8,128)} %param.5) | copy-start | bytes 49156
  0.6 4.1 %collective-permute-start = (f32[64,448]{1,0:T(8,128)}, f32[64,448]{1,0:T(8,128)S(1)}, u32[]{:S(2)}, u32[]{:S(2)}) collective-permute-start(f32[64,448]{1,0:T(8,128)} %bitcast.42), channel_id=1, source_target_pairs={{0,0},{1,1},{2,2},{3,3},{4,128},{5,129},{6,130},{7,131},{8,256},{9... | collective-permute-start | bytes 344072 | tf_op jit(solution)/shard_map/ppermute | solution.py:83
  4.7 45.0 %copy-start.1 = (f32[448,896]{1,0:T(8,128)S(1)}, f32[448,896]{1,0:T(8,128)}, u32[]{:S(2)}) copy-start(f32[448,896]{1,0:T(8,128)} %param.3) | copy-start | bytes 4816900
  4.8 45.0 %collective-permute-start.2 = (f32[64,448]{1,0:T(8,128)S(1)}, f32[64,448]{1,0:T(8,128)S(1)}, u32[]{:S(2)}, u32[]{:S(2)}) collective-permute-start(f32[64,448]{1,0:T(8,128)S(1)} %collective-permute-done), channel_id=1, source_target_pairs={{0,0},{1,32},{2,64},{3,96},{128,128},{129,160},{130,192},{131,224}... | collective-permute-start | bytes 344072 | tf_op jit(solution)/shard_map/ppermute | solution.py:87
  12.1 37.6 %collective-permute-start.1 = (f32[64,448]{1,0:T(8,128)S(1)}, f32[64,448]{1,0:T(8,128)S(1)}, u32[]{:S(2)}, u32[]{:S(2)}) collective-permute-start(f32[64,448]{1,0:T(8,128)S(1)} %collective-permute-done), channel_id=1, source_target_pairs={{0,16},{1,48},{2,80},{3,112},{128,144},{129,176},{130,208},{131,24... | collective-permute-start | bytes 344072 | tf_op jit(solution)/shard_map/ppermute | solution.py:87
  39.6 19.1 %all-to-all-start = ((f32[8,8,896]{2,1,0:T(8,128)}), f32[8,8,896]{2,1,0:T(8,128)S(1)}, u32[]{:S(2)}, u32[]{:S(2)}) async-start(f32[8,8,896]{2,1,0:T(8,128)} %bitcast.2), calls=%async_computation | async-start | bytes 458752 | tf_op jit(solution)/shard_map/all_to_all | solution.py:34
  90.6 31.8 %copy-start.2 = (f32[1,64,448]{2,1,0:T(8,128)S(1)}, f32[1,64,448]{2,1,0:T(8,128)}, u32[]{:S(2)}) copy-start(f32[1,64,448]{2,1,0:T(8,128)} %param.4) | copy-start | bytes 344068
  125.5 2.7 %copy-start.3 = (f32[64,448]{1,0:T(8,128)}, f32[64,448]{1,0:T(8,128)S(1)}, u32[]{:S(2)}) copy-start(f32[64,448]{1,0:T(8,128)S(1)} %fusion.2) | copy-start | bytes 344068

commit v5 on v4

--- a/solution.py
+++ b/solution.py
@@ -33,6 +33,16 @@
     chunks = values.reshape((parts, values.shape[0] // parts) + values.shape[1:])
     mine = jnp.sum(lax.all_to_all(chunks, axis, 0, 0, tiled=False), axis=0)
     return lax.all_gather(mine, axis, tiled=True)
+
+
+def scattered_sum_nested(values, axes):
+    if not axes:
+        return values
+    parts = lax.axis_size(axes[0])
+    chunks = values.reshape((parts, values.shape[0] // parts) + values.shape[1:])
+    mine = jnp.sum(lax.all_to_all(chunks, axes[0], 0, 0, tiled=False), axis=0)
+    mine = scattered_sum_nested(mine, axes[1:])
+    return lax.all_gather(mine, axes[0], tiled=True)
 
 
 def halves_sum(values, axis):
@@ -104,7 +114,7 @@
         factor = factors[0]
         row_index = lax.axis_index(tuple(row_axes))
         v_cols = to_column_blocks(v_rows, rows, cols, all_axes, row_index)
-        col_sums = scattered_sum(gathered_sum(contract(v_rows, current, 1, 0), row_axes[:1]), row_axes[1], lax.axis_size(row_axes[1]))
+        col_sums = scattered_sum_nested(gathered_sum(contract(v_rows, current, 1, 0), row_axes[:1]), row_axes[:0:-1])
         partial_value = contract(v_cols, current, 1, 1)
         partial_inner = contract(v_cols, col_sums, 1, 1)
         width = partial_value.shape[1]
@@ -124,14 +134,9 @@
 
 
 def solution(mesh):
-    row_axes, col_axes = ("x", "z"), ("y", "core")
     rows, cols = mesh.shape["row"], mesh.shape["col"]
-    split = (4, rows // 4, cols // 2, 2) if rows % 4 == 0 and cols % 2 == 0 else None
-    if split is None:
-        row_axes, col_axes = ("row",), ("col",)
-        fine = mesh
-    else:
-        fine = Mesh(mesh.devices.reshape(split), row_axes + col_axes)
+    row_axes, col_axes = ("x", "za", "zb"), ("y", "core")
+    fine = Mesh(mesh.devices.reshape((4, rows // 8, 2, cols // 2, 2)), row_axes + col_axes)
     return jax.shard_map(
         make_shards(row_axes, col_axes, rows, cols),
         mesh=fine,

time: 129 us -> 127 us (0.984)
  blocking collectives: 84.7 us -> 81.6 us
  starting transfers between devices: 22.7 us -> 25.5 us
  waiting for transfers between devices: 7.28 us -> 5.47 us
    all_to_all x1 -> x2, starting transfers between devices: 10.1 us -> 13.3 us  [scattered_sum_nested(): mine = jnp.sum(lax.all_to_all(chunks, axes[0], 0, 0, tiled=False), axis=0)]
    all_gather x1 -> x2, blocking collectives: 18.9 us -> 16.9 us  [scattered_sum_nested(): return lax.all_gather(mine, axes[0], tiled=True)]
    all_to_all x1 -> x2, waiting for transfers between devices: 7.27 us -> 5.46 us  [scattered_sum_nested(): mine = jnp.sum(lax.all_to_all(chunks, axes[0], 0, 0, tiled=False), axis=0)]
  transfers between devices with their start and end apart: 4 -> 5, of which waited for: 1 -> 1; matrix products, arithmetic and copies ran while one was open for 4% -> 2% of each run, Pallas kernels for 0% -> 0%
where the time goes in v5:
time: 127 us
  blocking collectives  81.6 us (64%)
  starting transfers between devices  25.5 us (20%)
  matrix products  11.7 us (9%)
  waiting for transfers between devices  5.47 us (4%)
  other arithmetic  1.58 us (1%)
    all_gather x3, blocking collectives, gathered_sum(): values = jnp.sum(lax.all_gather(values, axis), axis=0)  56.6 us
    all_gather x2, blocking collectives, scattered_sum_nested(): return lax.all_gather(mine, axes[0], tiled=True)  16.9 us
    all_to_all x2, starting transfers between devices, scattered_sum_nested(): mine = jnp.sum(lax.all_to_all(chunks, axes[0], 0, 0, tiled=False), axis=0)  13.3 us
    dot_general x11, matrix products, contract(): lax.dot_general(left_side, right_side, (((left_dim,), (right_dim,)), ((),...  11.7 us
    ppermute x2, starting transfers between devices, to_column_blocks(): lax.ppermute(moved, all_axes, [(mid, final[i]) for i, mid in first])  11.6 us
    all_gather x1, blocking collectives, split_sum(): both = lax.all_gather(total, split_axis)  8.06 us
    all_to_all x2, waiting for transfers between devices, scattered_sum_nested(): mine = jnp.sum(lax.all_to_all(chunks, axes[0], 0, 0, tiled=False), axis=0)  5.46 us
  transfers between devices with their start and end apart: 5, of which 1 were waited for; matrix products, arithmetic and copies ran while one was open for 2% of the time, Pallas kernels for 0%

profile of v5, /device:TPU:1, one launch (start us, length us, event | category | flops | bytes accessed | tf_op | source)
XLA Modules:
  0.0 126.8 jit_solution(4406974008919464624)
XLA Ops:
  0.6 2.5 %fusion.21 = f32[64,896]{1,0:T(8,128)S(1)} fusion(f32[448,896]{1,0:T(8,128)} %param.3, f32[1,64,448]{2,1,0:T(8,128)} %param.4), kind=kOutput, calls=%fused_computation.32 | convolution fusion | flops 308281344 | bytes 1949696 | tf_op jit(solution)/shard_map/dot_general | solution.py:9
  3.2 12.5 %all-gather = f32[256,896]{1,0:T(8,128)S(1)} all-gather(f32[64,896]{1,0:T(8,128)S(1)} %fusion.21), channel_id=2, replica_groups=mesh['x'=4,'za'=4,'zb'=2,'y'=8,'core'=2] {'x'}, dimensions={0}, use_global_device_ids=true | all-gather | bytes 1146880 | tf_op jit(solution)/shard_map/all_gather | solution.py:20
  15.7 0.7 reduce_sum.45
  16.5 4.4 %all-to-all-start = ((f32[2,32,896]{2,1,0:T(8,128)}), f32[2,32,896]{2,1,0:T(8,128)S(1)}, u32[]{:S(2)}, u32[]{:S(2)}) async-start(f32[2,32,896]{2,1,0:T(8,128)} %bitcast.2), calls=%async_computation | async-start | bytes 458752 | tf_op jit(solution)/shard_map/all_to_all | solution.py:43
  20.9 0.7 collective-permute-start
  21.6 8.0 %collective-permute-start.2 = (f32[64,448]{1,0:T(8,128)S(1)}, f32[64,448]{1,0:T(8,128)S(1)}, u32[]{:S(2)}, u32[]{:S(2)}) collective-permute-start(f32[64,448]{1,0:T(8,128)S(1)} %collective-permute-done), channel_id=1, source_target_pairs={{0,0},{1,32},{2,64},{3,96},{128,128},{129,160},{130,192},{131,224}... | collective-permute-start | bytes 344072 | tf_op jit(solution)/shard_map/ppermute | solution.py:97
  29.6 3.5 %collective-permute-start.1 = (f32[64,448]{1,0:T(8,128)S(1)}, f32[64,448]{1,0:T(8,128)S(1)}, u32[]{:S(2)}, u32[]{:S(2)}) collective-permute-start(f32[64,448]{1,0:T(8,128)S(1)} %collective-permute-done), channel_id=1, source_target_pairs={{0,16},{1,48},{2,80},{3,112},{128,144},{129,176},{130,208},{131,24... | collective-permute-start | bytes 344072 | tf_op jit(solution)/shard_map/ppermute | solution.py:97
  33.2 0.7 reduce_sum.46
  33.9 8.9 %all-to-all-start.1 = ((f32[4,8,896]{2,1,0:T(8,128)}), f32[4,8,896]{2,1,0:T(8,128)S(1)}, u32[]{:S(2)}, u32[]{:S(2)}) async-start(f32[4,8,896]{2,1,0:T(8,128)} %bitcast.3), calls=%async_computation.1 | async-start | bytes 229376 | tf_op jit(solution)/shard_map/all_to_all | solution.py:43
  42.8 1.7 %fusion.5 = f32[64,448]{1,0:T(8,128)S(1)} fusion(f32[448,896]{1,0:T(8,128)S(1)} %copy-done.1, f32[64,448]{1,0:T(8,128)S(1)} %get-tuple-element.3, f32[64,448]{1,0:T(8,128)S(1)} %get-tuple-element.2), kind=kOutput, calls=%fused_computation.16 | convolution fusion | flops 308338688 | bytes 1949696 | tf_op jit(solution)/shard_map/dot_general | solution.py:9
  44.5 5.5 %all-to-all-done.1 = f32[4,8,896]{2,1,0:T(8,128)S(1)} async-done(((f32[4,8,896]{2,1,0:T(8,128)}), f32[4,8,896]{2,1,0:T(8,128)S(1)}, u32[]{:S(2)}, u32[]{:S(2)}) %all-to-all-start.1) | async-done | bytes 114720 | tf_op jit(solution)/shard_map/all_to_all | solution.py:43
  49.9 12.2 %all_gather.32 = f32[32,896]{1,0:T(8,128)S(1)} all-gather(f32[8,896]{1,0:T(8,128)S(1)} %reduce_sum.47), channel_id=1, replica_groups=mesh['x'=4,'za'=4,'zb'=2,'y'=8,'core'=2] {'za'}, dimensions={0}, use_global_device_ids=true | all-gather | bytes 143360 | tf_op jit(solution)/shard_map/all_gather | solution.py:45
  62.1 4.8 %all_gather.33 = f32[64,896]{1,0:T(8,128)S(1)} all-gather(f32[32,896]{1,0:T(8,128)S(1)} %all_gather.32), channel_id=1, replica_groups=mesh['x'=4,'za'=4,'zb'=2,'y'=8,'core'=2] {'zb'}, dimensions={0}, use_global_device_ids=true | all-gather | bytes 344064 | tf_op jit(solution)/shard_map/all_gather | solution.py:45
  66.9 0.4 fusion.4
  67.3 8.3 %all-gather.1 = f32[128,512]{1,0:T(8,128)S(1)} all-gather(f32[64,512]{1,0:T(8,128)S(1)} %pad_maximum_fusion.3), channel_id=3, replica_groups=mesh['x'=4,'za'=4,'zb'=2,'y'=8,'core'=2] {'core'}, dimensions={0}, use_global_device_ids=true | all-gather | bytes 393216 | tf_op jit(solution)/shard_map/all_gather | solution.py:20
  75.7 0.9 convolution_bitcast_fusion
  76.6 35.7 %all-gather.2 = f32[512,256]{1,0:T(8,128)S(1)} all-gather(f32[64,256]{1,0:T(8,128)S(1)} %slice_select_fusion), channel_id=4, replica_groups=mesh['x'=4,'za'=4,'zb'=2,'y'=8,'core'=2] {'y'}, dimensions={0}, use_global_device_ids=true | all-gather | bytes 589824 | tf_op jit(solution)/shard_map/all_gather | solution.py:20
  112.4 8.1 %all-gather.3 = f32[128,256]{1,0:T(8,128)S(1)} all-gather(f32[64,256]{1,0:T(8,128)S(1)} %reduce_sum.49), channel_id=5, replica_groups=mesh['x'=4,'za'=4,'zb'=2,'y'=8,'core'=2] {'core'}, dimensions={0}, use_global_device_ids=true | all-gather | bytes 196608 | tf_op jit(solution)/shard_map/all_gather | solution.py:28
  120.5 0.3 fusion.6
  121.0 0.3 convolution_multiply_fusion.1
  121.3 1.0 fusion.1
  122.3 1.5 %fusion.19 = f32[896,448]{0,1:T(8,128)S(1)} fusion(f32[64,896]{0,1:T(8,128)S(1)} %fusion.1, f32[1,64,448]{2,1,0:T(8,128)S(1)} %copy-done.2), kind=kOutput, calls=%fused_computation.30 | convolution fusion | flops 308281344 | bytes 1949696 | tf_op jit(solution)/shard_map/dot_general | solution.py:9
  123.8 0.3 fusion.2
  124.1 2.6 %fusion = f32[448,896]{1,0:T(8,128)} fusion(f32[448,896]{1,0:T(8,128)S(1)} %copy-done.1, f32[896,448]{0,1:T(8,128)S(1)} %fusion.19, f32[64,448]{1,0:T(8,128)S(1)} %fusion.2, f32[64,448]{1,0:T(8,128)S(1)} %get-tuple-element.3, f32[64,448]{1,0:T(8,128)S(1)} %get-tuple-element.2), kind=kOutput, calls=%fused_computation.1 | convolution fusion | flops 309141504 | bytes 5160960 | tf_op jit(solution)/shard_map/dot_general | solution.py:9
  (20 shorter events, 0.5 us)
Async XLA Ops:
  0.6 75.1 %copy-start = (f32[1,64,64]{2,1,0:T(8,128)S(1)}, f32[1,64,64]{2,1,0:T(8,128)}, u32[]{:S(2)}) copy-start(f32[1,64,64]{2,1,0:T(8,128)} %param.5) | copy-start | bytes 49156
  3.2 17.7 %copy-start.2 = (f32[1,64,448]{2,1,0:T(8,128)S(1)}, f32[1,64,448]{2,1,0:T(8,128)}, u32[]{:S(2)}) copy-start(f32[1,64,448]{2,1,0:T(8,128)} %param.4) | copy-start | bytes 344068
  15.7 27.1 %copy-start.1 = (f32[448,896]{1,0:T(8,128)S(1)}, f32[448,896]{1,0:T(8,128)}, u32[]{:S(2)}) copy-start(f32[448,896]{1,0:T(8,128)} %param.3) | copy-start | bytes 4816900
  16.5 16.7 %all-to-all-start = ((f32[2,32,896]{2,1,0:T(8,128)}), f32[2,32,896]{2,1,0:T(8,128)S(1)}, u32[]{:S(2)}, u32[]{:S(2)}) async-start(f32[2,32,896]{2,1,0:T(8,128)} %bitcast.2), calls=%async_computation | async-start | bytes 458752 | tf_op jit(solution)/shard_map/all_to_all | solution.py:43
  20.9 0.7 collective-permute-start
  21.6 21.2 %collective-permute-start.2 = (f32[64,448]{1,0:T(8,128)S(1)}, f32[64,448]{1,0:T(8,128)S(1)}, u32[]{:S(2)}, u32[]{:S(2)}) collective-permute-start(f32[64,448]{1,0:T(8,128)S(1)} %collective-permute-done), channel_id=1, source_target_pairs={{0,0},{1,32},{2,64},{3,96},{128,128},{129,160},{130,192},{131,224}... | collective-permute-start | bytes 344072 | tf_op jit(solution)/shard_map/ppermute | solution.py:97
  29.6 13.2 %collective-permute-start.1 = (f32[64,448]{1,0:T(8,128)S(1)}, f32[64,448]{1,0:T(8,128)S(1)}, u32[]{:S(2)}, u32[]{:S(2)}) collective-permute-start(f32[64,448]{1,0:T(8,128)S(1)} %collective-permute-done), channel_id=1, source_target_pairs={{0,16},{1,48},{2,80},{3,112},{128,144},{129,176},{130,208},{131,24... | collective-permute-start | bytes 344072 | tf_op jit(solution)/shard_map/ppermute | solution.py:97
  33.9 16.0 %all-to-all-start.1 = ((f32[4,8,896]{2,1,0:T(8,128)}), f32[4,8,896]{2,1,0:T(8,128)S(1)}, u32[]{:S(2)}, u32[]{:S(2)}) async-start(f32[4,8,896]{2,1,0:T(8,128)} %bitcast.3), calls=%async_computation.1 | async-start | bytes 229376 | tf_op jit(solution)/shard_map/all_to_all | solution.py:43
  124.1 2.7 %copy-start.3 = (f32[64,448]{1,0:T(8,128)}, f32[64,448]{1,0:T(8,128)S(1)}, u32[]{:S(2)}) copy-start(f32[64,448]{1,0:T(8,128)S(1)} %fusion.2) | copy-start | bytes 344068

commit v6 on v5

--- a/solution.py
+++ b/solution.py
@@ -5,14 +5,18 @@
 from jax.sharding import PartitionSpec as P
 
 
-def contract(left_side, right_side, left_dim, right_dim):
+def contract(left_side, right_side, left_dim, right_dim, precision=lax.Precision.HIGHEST):
     return lax.dot_general(
         left_side,
         right_side,
         (((left_dim,), (right_dim,)), ((), ())),
-        precision=lax.Precision.HIGHEST,
+        precision=precision,
         preferred_element_type=jnp.float32,
     )
+
+
+def contract_matrix(left_side, right_side, left_dim, right_dim):
+    return contract(left_side, right_side, left_dim, right_dim, lax.Precision.HIGH)
 
 
 def gathered_sum(values, axes):
@@ -35,13 +39,13 @@
     return lax.all_gather(mine, axis, tiled=True)
 
 
-def scattered_sum_nested(values, axes):
+def scattered_sum_nested(values, axes, inner_axes=()):
     if not axes:
-        return values
+        return gathered_sum(values, inner_axes)
     parts = lax.axis_size(axes[0])
     chunks = values.reshape((parts, values.shape[0] // parts) + values.shape[1:])
     mine = jnp.sum(lax.all_to_all(chunks, axes[0], 0, 0, tiled=False), axis=0)
-    mine = scattered_sum_nested(mine, axes[1:])
+    mine = scattered_sum_nested(mine, axes[1:], inner_axes)
     return lax.all_gather(mine, axes[0], tiled=True)
 
 
@@ -114,8 +118,8 @@
         factor = factors[0]
         row_index = lax.axis_index(tuple(row_axes))
         v_cols = to_column_blocks(v_rows, rows, cols, all_axes, row_index)
-        col_sums = scattered_sum_nested(gathered_sum(contract(v_rows, current, 1, 0), row_axes[:1]), row_axes[:0:-1])
-        partial_value = contract(v_cols, current, 1, 1)
+        col_sums = scattered_sum_nested(contract_matrix(v_rows, current, 1, 0), row_axes[:0:-1], row_axes[:1])
+        partial_value = contract_matrix(v_cols, current, 1, 1)
         partial_inner = contract(v_cols, col_sums, 1, 1)
         width = partial_value.shape[1]
         sums = split_sum(gathered_sum(jnp.concatenate([partial_value, partial_inner], axis=1), col_axes[1:]), col_axes[0], col_axes[1])
@@ -127,7 +131,7 @@
         mixing = contract(projected, factor, 0, 0)
         w_rows = x_rows - 0.5 * contract(mixing, v_rows, 1, 0)
         w_cols = x_cols - 0.5 * contract(mixing, v_cols, 1, 0)
-        current = current - contract(v_rows, w_cols, 0, 0) - contract(w_rows, v_cols, 0, 0)
+        current = current - contract_matrix(v_rows, w_cols, 0, 0) - contract_matrix(w_rows, v_cols, 0, 0)
         return (current, jnp.stack([w_rows]))
 
     return shards

time: 127 us -> 125 us (0.984)
  matrix products: 11.7 us -> 10 us
  waiting for transfers between devices: 5.47 us -> 6.75 us
    dot_general x11, matrix products: 11.7 us -> 10 us  [contract(): lax.dot_general(left_side, right_side, (((left_dim,), (right_dim,)), ((),...]
    all_gather x2, blocking collectives: 16.9 us -> 15.3 us  [scattered_sum_nested(): return lax.all_gather(mine, axes[0], tiled=True)]
    ppermute x2, starting transfers between devices: 11.6 us -> 10.2 us  [to_column_blocks(): lax.ppermute(moved, all_axes, [(mid, final[i]) for i, mid in first])]
    all_to_all x2, waiting for transfers between devices: 5.46 us -> 6.74 us  [scattered_sum_nested(): mine = jnp.sum(lax.all_to_all(chunks, axes[0], 0, 0, tiled=False), axis=0)]
  transfers between devices with their start and end apart: 5 -> 5, of which waited for: 1 -> 1; matrix products, arithmetic and copies ran while one was open for 2% -> 1% of each run, Pallas kernels for 0% -> 0%
where the time goes in v6:
time: 125 us; the launch traced here: 124 us
  blocking collectives  80.5 us (64%)
  starting transfers between devices  25.3 us (20%)
  matrix products  10 us (8%)
  waiting for transfers between devices  6.75 us (5%)
    all_gather x3, blocking collectives, gathered_sum(): values = jnp.sum(lax.all_gather(values, axis), axis=0)  57.1 us
    all_gather x2, blocking collectives, scattered_sum_nested(): return lax.all_gather(mine, axes[0], tiled=True)  15.3 us
    all_to_all x2, starting transfers between devices, scattered_sum_nested(): mine = jnp.sum(lax.all_to_all(chunks, axes[0], 0, 0, tiled=False), axis=0)  14.4 us
    ppermute x2, starting transfers between devices, to_column_blocks(): lax.ppermute(moved, all_axes, [(mid, final[i]) for i, mid in first])  10.2 us
    dot_general x11, matrix products, contract(): lax.dot_general(left_side, right_side, (((left_dim,), (right_dim,)), ((),...  10 us
    all_gather x1, blocking collectives, split_sum(): both = lax.all_gather(total, split_axis)  8.06 us
    all_to_all x2, waiting for transfers between devices, scattered_sum_nested(): mine = jnp.sum(lax.all_to_all(chunks, axes[0], 0, 0, tiled=False), axis=0)  6.74 us
  transfers between devices with their start and end apart: 5, of which 1 were waited for; matrix products, arithmetic and copies ran while one was open for 1% of the time, Pallas kernels for 0%

profile of v6, /device:TPU:1, one launch (start us, length us, event | category | flops | bytes accessed | tf_op | source)
XLA Modules:
  0.0 124.3 jit_solution(12636825838351279103)
XLA Ops:
  0.7 2.9 %fusion.1 = f32[2,32,896]{2,1,0:T(8,128)} fusion(f32[2,32,448]{2,1,0:T(8,128)} %bitcast.44, f32[448,896]{1,0:T(8,128)} %param.3), kind=kOutput, calls=%fused_computation.2 | convolution fusion | flops 154140672 | bytes 1949696 | tf_op jit(solution)/shard_map/dot_general | solution.py:9
  3.5 4.2 %all-to-all-start = ((f32[2,32,896]{2,1,0:T(8,128)}), f32[2,32,896]{2,1,0:T(8,128)S(1)}, u32[]{:S(2)}, u32[]{:S(2)}) async-start(f32[2,32,896]{2,1,0:T(8,128)} %fusion.1), calls=%async_computation | async-start | bytes 458752 | tf_op jit(solution)/shard_map/all_to_all | solution.py:47
  7.7 0.7 collective-permute-start
  8.4 6.7 %collective-permute-start.2 = (f32[64,448]{1,0:T(8,128)S(1)}, f32[64,448]{1,0:T(8,128)S(1)}, u32[]{:S(2)}, u32[]{:S(2)}) collective-permute-start(f32[64,448]{1,0:T(8,128)S(1)} %collective-permute-done), channel_id=1, source_target_pairs={{0,0},{1,32},{2,64},{3,96},{128,128},{129,160},{130,192},{131,224}... | collective-permute-start | bytes 344072 | tf_op jit(solution)/shard_map/ppermute | solution.py:101
  15.1 3.5 %collective-permute-start.1 = (f32[64,448]{1,0:T(8,128)S(1)}, f32[64,448]{1,0:T(8,128)S(1)}, u32[]{:S(2)}, u32[]{:S(2)}) collective-permute-start(f32[64,448]{1,0:T(8,128)S(1)} %collective-permute-done), channel_id=1, source_target_pairs={{0,16},{1,48},{2,80},{3,112},{128,144},{129,176},{130,208},{131,24... | collective-permute-start | bytes 344072 | tf_op jit(solution)/shard_map/ppermute | solution.py:101
  18.7 0.7 reduce_sum.45
  19.3 10.3 %all-to-all-start.1 = ((f32[4,8,896]{2,1,0:T(8,128)}), f32[4,8,896]{2,1,0:T(8,128)S(1)}, u32[]{:S(2)}, u32[]{:S(2)}) async-start(f32[4,8,896]{2,1,0:T(8,128)} %bitcast.2), calls=%async_computation.1 | async-start | bytes 229376 | tf_op jit(solution)/shard_map/all_to_all | solution.py:47
  29.7 0.9 fusion.7
  30.5 6.7 %all-to-all-done.1 = f32[4,8,896]{2,1,0:T(8,128)S(1)} async-done(((f32[4,8,896]{2,1,0:T(8,128)}), f32[4,8,896]{2,1,0:T(8,128)S(1)}, u32[]{:S(2)}, u32[]{:S(2)}) %all-to-all-start.1) | async-done | bytes 114720 | tf_op jit(solution)/shard_map/all_to_all | solution.py:47
  37.3 22.4 %all-gather = f32[32,896]{1,0:T(8,128)S(1)} all-gather(f32[8,896]{1,0:T(8,128)S(1)} %reduce_sum.46), channel_id=2, replica_groups=mesh['x'=4,'za'=4,'zb'=2,'y'=8,'core'=2] {'x'}, dimensions={0}, use_global_device_ids=true | all-gather | bytes 143360 | tf_op jit(solution)/shard_map/all_gather | solution.py:24
  59.7 11.0 %all_gather.32 = f32[32,896]{1,0:T(8,128)S(1)} all-gather(f32[8,896]{1,0:T(8,128)S(1)} %bitcast_reduce_fusion), channel_id=1, replica_groups=mesh['x'=4,'za'=4,'zb'=2,'y'=8,'core'=2] {'za'}, dimensions={0}, use_global_device_ids=true | all-gather | bytes 143360 | tf_op jit(solution)/shard_map/all_gather | solution.py:49
  70.7 4.3 %all_gather.33 = f32[64,896]{1,0:T(8,128)S(1)} all-gather(f32[32,896]{1,0:T(8,128)S(1)} %all_gather.32), channel_id=1, replica_groups=mesh['x'=4,'za'=4,'zb'=2,'y'=8,'core'=2] {'zb'}, dimensions={0}, use_global_device_ids=true | all-gather | bytes 344064 | tf_op jit(solution)/shard_map/all_gather | solution.py:49
  75.0 0.4 fusion.6
  75.5 11.5 %all-gather.1 = f32[128,512]{1,0:T(8,128)S(1)} all-gather(f32[64,512]{1,0:T(8,128)S(1)} %pad_maximum_fusion.3), channel_id=3, replica_groups=mesh['x'=4,'za'=4,'zb'=2,'y'=8,'core'=2] {'core'}, dimensions={0}, use_global_device_ids=true | all-gather | bytes 393216 | tf_op jit(solution)/shard_map/all_gather | solution.py:24
  87.0 0.9 convolution_bitcast_fusion
  88.0 23.2 %all-gather.2 = f32[512,256]{1,0:T(8,128)S(1)} all-gather(f32[64,256]{1,0:T(8,128)S(1)} %slice_select_fusion), channel_id=4, replica_groups=mesh['x'=4,'za'=4,'zb'=2,'y'=8,'core'=2] {'y'}, dimensions={0}, use_global_device_ids=true | all-gather | bytes 589824 | tf_op jit(solution)/shard_map/all_gather | solution.py:24
  111.2 8.1 %all-gather.3 = f32[128,256]{1,0:T(8,128)S(1)} all-gather(f32[64,256]{1,0:T(8,128)S(1)} %reduce_sum.49), channel_id=5, replica_groups=mesh['x'=4,'za'=4,'zb'=2,'y'=8,'core'=2] {'core'}, dimensions={0}, use_global_device_ids=true | all-gather | bytes 196608 | tf_op jit(solution)/shard_map/all_gather | solution.py:32
  119.2 0.3 fusion.8
  119.6 0.2 fusion.11
  119.8 0.3 convolution_multiply_fusion.1
  120.1 1.0 fusion.3
  121.1 0.8 fusion.21
  121.9 0.3 fusion.4
  122.2 2.1 %fusion = f32[448,896]{1,0:T(8,128)} fusion(f32[448,896]{1,0:T(8,128)S(1)} %copy-done.1, f32[896,448]{0,1:T(8,128)S(1)} %fusion.21, f32[64,448]{1,0:T(8,128)S(1)} %fusion.4, f32[64,448]{1,0:T(8,128)S(1)} %get-tuple-element.3, f32[64,448]{1,0:T(8,128)S(1)} %get-tuple-element.2), kind=kOutput, calls=%fused_computation.1 | convolution fusion | flops 155000832 | bytes 5160960 | tf_op jit(solution)/shard_map/dot_general | solution.py:9
  (20 shorter events, 0.2 us)
Async XLA Ops:
  0.6 86.4 %copy-start = (f32[1,64,64]{2,1,0:T(8,128)S(1)}, f32[1,64,64]{2,1,0:T(8,128)}, u32[]{:S(2)}) copy-start(f32[1,64,64]{2,1,0:T(8,128)} %param.5) | copy-start | bytes 49156
  0.6 7.1 %copy-start.2 = (f32[1,64,448]{2,1,0:T(8,128)S(1)}, f32[1,64,448]{2,1,0:T(8,128)}, u32[]{:S(2)}) copy-start(f32[1,64,448]{2,1,0:T(8,128)} %param.4) | copy-start | bytes 344068
  0.7 29.0 %copy-start.1 = (f32[448,896]{1,0:T(8,128)S(1)}, f32[448,896]{1,0:T(8,128)}, u32[]{:S(2)}) copy-start(f32[448,896]{1,0:T(8,128)} %param.3) | copy-start | bytes 4816900
  3.5 15.1 %all-to-all-start = ((f32[2,32,896]{2,1,0:T(8,128)}), f32[2,32,896]{2,1,0:T(8,128)S(1)}, u32[]{:S(2)}, u32[]{:S(2)}) async-start(f32[2,32,896]{2,1,0:T(8,128)} %fusion.1), calls=%async_computation | async-start | bytes 458752 | tf_op jit(solution)/shard_map/all_to_all | solution.py:47
  7.7 0.7 collective-permute-start
  8.4 21.2 %collective-permute-start.2 = (f32[64,448]{1,0:T(8,128)S(1)}, f32[64,448]{1,0:T(8,128)S(1)}, u32[]{:S(2)}, u32[]{:S(2)}) collective-permute-start(f32[64,448]{1,0:T(8,128)S(1)} %collective-permute-done), channel_id=1, source_target_pairs={{0,0},{1,32},{2,64},{3,96},{128,128},{129,160},{130,192},{131,224}... | collective-permute-start | bytes 344072 | tf_op jit(solution)/shard_map/ppermute | solution.py:101
  15.1 14.5 %collective-permute-start.1 = (f32[64,448]{1,0:T(8,128)S(1)}, f32[64,448]{1,0:T(8,128)S(1)}, u32[]{:S(2)}, u32[]{:S(2)}) collective-permute-start(f32[64,448]{1,0:T(8,128)S(1)} %collective-permute-done), channel_id=1, source_target_pairs={{0,16},{1,48},{2,80},{3,112},{128,144},{129,176},{130,208},{131,24... | collective-permute-start | bytes 344072 | tf_op jit(solution)/shard_map/ppermute | solution.py:101
  19.3 17.9 %all-to-all-start.1 = ((f32[4,8,896]{2,1,0:T(8,128)}), f32[4,8,896]{2,1,0:T(8,128)S(1)}, u32[]{:S(2)}, u32[]{:S(2)}) async-start(f32[4,8,896]{2,1,0:T(8,128)} %bitcast.2), calls=%async_computation.1 | async-start | bytes 229376 | tf_op jit(solution)/shard_map/all_to_all | solution.py:47
  122.2 2.1 %copy-start.3 = (f32[64,448]{1,0:T(8,128)}, f32[64,448]{1,0:T(8,128)S(1)}, u32[]{:S(2)}) copy-start(f32[64,448]{1,0:T(8,128)S(1)} %fusion.4) | copy-start | bytes 344068

commit v7 on v5

--- a/solution.py
+++ b/solution.py
@@ -35,13 +35,13 @@
     return lax.all_gather(mine, axis, tiled=True)
 
 
-def scattered_sum_nested(values, axes):
+def scattered_sum_nested(values, axes, inner_axes=()):
     if not axes:
-        return values
+        return gathered_sum(values, inner_axes)
     parts = lax.axis_size(axes[0])
     chunks = values.reshape((parts, values.shape[0] // parts) + values.shape[1:])
     mine = jnp.sum(lax.all_to_all(chunks, axes[0], 0, 0, tiled=False), axis=0)
-    mine = scattered_sum_nested(mine, axes[1:])
+    mine = scattered_sum_nested(mine, axes[1:], inner_axes)
     return lax.all_gather(mine, axes[0], tiled=True)
 
 
@@ -114,7 +114,7 @@
         factor = factors[0]
         row_index = lax.axis_index(tuple(row_axes))
         v_cols = to_column_blocks(v_rows, rows, cols, all_axes, row_index)
-        col_sums = scattered_sum_nested(gathered_sum(contract(v_rows, current, 1, 0), row_axes[:1]), row_axes[:0:-1])
+        col_sums = scattered_sum_nested(contract(v_rows, current, 1, 0), row_axes[:0:-1], row_axes[:1])
         partial_value = contract(v_cols, current, 1, 1)
         partial_inner = contract(v_cols, col_sums, 1, 1)
         width = partial_value.shape[1]

time: 127 us -> 126 us (level)
    all_gather x2, blocking collectives: 16.9 us -> 15.3 us  [scattered_sum_nested(): return lax.all_gather(mine, axes[0], tiled=True)]
    ppermute x2, starting transfers between devices: 11.6 us -> 10.2 us  [to_column_blocks(): lax.ppermute(moved, all_axes, [(mid, final[i]) for i, mid in first])]
where the time goes in v7:
time: 126 us
  blocking collectives  80.5 us (64%)
  starting transfers between devices  25.3 us (20%)
  matrix products  12.5 us (10%)
  waiting for transfers between devices  5.96 us (5%)
    all_gather x3, blocking collectives, gathered_sum(): values = jnp.sum(lax.all_gather(values, axis), axis=0)  57.1 us
    all_gather x2, blocking collectives, scattered_sum_nested(): return lax.all_gather(mine, axes[0], tiled=True)  15.3 us
    all_to_all x2, starting transfers between devices, scattered_sum_nested(): mine = jnp.sum(lax.all_to_all(chunks, axes[0], 0, 0, tiled=False), axis=0)  14.4 us
    dot_general x11, matrix products, contract(): lax.dot_general(left_side, right_side, (((left_dim,), (right_dim,)), ((),...  12.5 us
    ppermute x2, starting transfers between devices, to_column_blocks(): lax.ppermute(moved, all_axes, [(mid, final[i]) for i, mid in first])  10.2 us
    all_gather x1, blocking collectives, split_sum(): both = lax.all_gather(total, split_axis)  8.06 us
    all_to_all x2, waiting for transfers between devices, scattered_sum_nested(): mine = jnp.sum(lax.all_to_all(chunks, axes[0], 0, 0, tiled=False), axis=0)  5.96 us
  transfers between devices with their start and end apart: 5, of which 1 were waited for; matrix products, arithmetic and copies ran while one was open for 2% of the time, Pallas kernels for 0%

profile of v7, /device:TPU:1, one launch (start us, length us, event | category | flops | bytes accessed | tf_op | source)
XLA Modules:
  0.0 126.0 jit_solution(15985915384747517785)
XLA Ops:
  0.7 3.3 %fusion.1 = f32[2,32,896]{2,1,0:T(8,128)} fusion(f32[2,32,448]{2,1,0:T(8,128)} %bitcast.44, f32[448,896]{1,0:T(8,128)} %param.3), kind=kOutput, calls=%fused_computation.2 | convolution fusion | flops 308281344 | bytes 1949696 | tf_op jit(solution)/shard_map/dot_general | solution.py:9
  4.0 4.2 %all-to-all-start = ((f32[2,32,896]{2,1,0:T(8,128)}), f32[2,32,896]{2,1,0:T(8,128)S(1)}, u32[]{:S(2)}, u32[]{:S(2)}) async-start(f32[2,32,896]{2,1,0:T(8,128)} %fusion.1), calls=%async_computation | async-start | bytes 458752 | tf_op jit(solution)/shard_map/all_to_all | solution.py:43
  8.2 0.7 collective-permute-start
  8.9 6.7 %collective-permute-start.2 = (f32[64,448]{1,0:T(8,128)S(1)}, f32[64,448]{1,0:T(8,128)S(1)}, u32[]{:S(2)}, u32[]{:S(2)}) collective-permute-start(f32[64,448]{1,0:T(8,128)S(1)} %collective-permute-done), channel_id=1, source_target_pairs={{0,0},{1,32},{2,64},{3,96},{128,128},{129,160},{130,192},{131,224}... | collective-permute-start | bytes 344072 | tf_op jit(solution)/shard_map/ppermute | solution.py:97
  15.5 3.5 %collective-permute-start.1 = (f32[64,448]{1,0:T(8,128)S(1)}, f32[64,448]{1,0:T(8,128)S(1)}, u32[]{:S(2)}, u32[]{:S(2)}) collective-permute-start(f32[64,448]{1,0:T(8,128)S(1)} %collective-permute-done), channel_id=1, source_target_pairs={{0,16},{1,48},{2,80},{3,112},{128,144},{129,176},{130,208},{131,24... | collective-permute-start | bytes 344072 | tf_op jit(solution)/shard_map/ppermute | solution.py:97
  19.1 0.7 reduce_sum.45
  19.8 10.3 %all-to-all-start.1 = ((f32[4,8,896]{2,1,0:T(8,128)}), f32[4,8,896]{2,1,0:T(8,128)S(1)}, u32[]{:S(2)}, u32[]{:S(2)}) async-start(f32[4,8,896]{2,1,0:T(8,128)} %bitcast.2), calls=%async_computation.1 | async-start | bytes 229376 | tf_op jit(solution)/shard_map/all_to_all | solution.py:43
  30.1 1.7 %fusion.7 = f32[64,448]{1,0:T(8,128)S(1)} fusion(f32[448,896]{1,0:T(8,128)S(1)} %copy-done.1, f32[64,448]{1,0:T(8,128)S(1)} %get-tuple-element.3, f32[64,448]{1,0:T(8,128)S(1)} %get-tuple-element.2), kind=kOutput, calls=%fused_computation.19 | convolution fusion | flops 308338688 | bytes 1949696 | tf_op jit(solution)/shard_map/dot_general | solution.py:9
  31.8 6.0 %all-to-all-done.1 = f32[4,8,896]{2,1,0:T(8,128)S(1)} async-done(((f32[4,8,896]{2,1,0:T(8,128)}), f32[4,8,896]{2,1,0:T(8,128)S(1)}, u32[]{:S(2)}, u32[]{:S(2)}) %all-to-all-start.1) | async-done | bytes 114720 | tf_op jit(solution)/shard_map/all_to_all | solution.py:43
  37.7 22.4 %all-gather = f32[32,896]{1,0:T(8,128)S(1)} all-gather(f32[8,896]{1,0:T(8,128)S(1)} %reduce_sum.46), channel_id=2, replica_groups=mesh['x'=4,'za'=4,'zb'=2,'y'=8,'core'=2] {'x'}, dimensions={0}, use_global_device_ids=true | all-gather | bytes 143360 | tf_op jit(solution)/shard_map/all_gather | solution.py:20
  60.1 11.0 %all_gather.32 = f32[32,896]{1,0:T(8,128)S(1)} all-gather(f32[8,896]{1,0:T(8,128)S(1)} %bitcast_reduce_fusion), channel_id=1, replica_groups=mesh['x'=4,'za'=4,'zb'=2,'y'=8,'core'=2] {'za'}, dimensions={0}, use_global_device_ids=true | all-gather | bytes 143360 | tf_op jit(solution)/shard_map/all_gather | solution.py:45
  71.1 4.3 %all_gather.33 = f32[64,896]{1,0:T(8,128)S(1)} all-gather(f32[32,896]{1,0:T(8,128)S(1)} %all_gather.32), channel_id=1, replica_groups=mesh['x'=4,'za'=4,'zb'=2,'y'=8,'core'=2] {'zb'}, dimensions={0}, use_global_device_ids=true | all-gather | bytes 344064 | tf_op jit(solution)/shard_map/all_gather | solution.py:45
  75.4 0.4 fusion.6
  75.9 11.6 %all-gather.1 = f32[128,512]{1,0:T(8,128)S(1)} all-gather(f32[64,512]{1,0:T(8,128)S(1)} %pad_maximum_fusion.3), channel_id=3, replica_groups=mesh['x'=4,'za'=4,'zb'=2,'y'=8,'core'=2] {'core'}, dimensions={0}, use_global_device_ids=true | all-gather | bytes 393216 | tf_op jit(solution)/shard_map/all_gather | solution.py:20
  87.6 0.9 convolution_bitcast_fusion
  88.5 23.1 %all-gather.2 = f32[512,256]{1,0:T(8,128)S(1)} all-gather(f32[64,256]{1,0:T(8,128)S(1)} %slice_select_fusion), channel_id=4, replica_groups=mesh['x'=4,'za'=4,'zb'=2,'y'=8,'core'=2] {'y'}, dimensions={0}, use_global_device_ids=true | all-gather | bytes 589824 | tf_op jit(solution)/shard_map/all_gather | solution.py:20
  111.6 8.1 %all-gather.3 = f32[128,256]{1,0:T(8,128)S(1)} all-gather(f32[64,256]{1,0:T(8,128)S(1)} %reduce_sum.49), channel_id=5, replica_groups=mesh['x'=4,'za'=4,'zb'=2,'y'=8,'core'=2] {'core'}, dimensions={0}, use_global_device_ids=true | all-gather | bytes 196608 | tf_op jit(solution)/shard_map/all_gather | solution.py:28
  119.7 0.3 fusion.8
  120.0 0.2 fusion.11
  120.3 0.3 convolution_multiply_fusion.1
  120.5 1.0 fusion.3
  121.5 1.5 %fusion.21 = f32[896,448]{0,1:T(8,128)S(1)} fusion(f32[64,896]{0,1:T(8,128)S(1)} %fusion.3, f32[1,64,448]{2,1,0:T(8,128)S(1)} %copy-done.2), kind=kOutput, calls=%fused_computation.33 | convolution fusion | flops 308281344 | bytes 1949696 | tf_op jit(solution)/shard_map/dot_general | solution.py:9
  123.0 0.3 fusion.4
  123.3 2.6 %fusion = f32[448,896]{1,0:T(8,128)} fusion(f32[448,896]{1,0:T(8,128)S(1)} %copy-done.1, f32[896,448]{0,1:T(8,128)S(1)} %fusion.21, f32[64,448]{1,0:T(8,128)S(1)} %fusion.4, f32[64,448]{1,0:T(8,128)S(1)} %get-tuple-element.3, f32[64,448]{1,0:T(8,128)S(1)} %get-tuple-element.2), kind=kOutput, calls=%fused_computation.1 | convolution fusion | flops 309141504 | bytes 5160960 | tf_op jit(solution)/shard_map/dot_general | solution.py:9
  (20 shorter events, 0.2 us)
Async XLA Ops:
  0.6 87.0 %copy-start = (f32[1,64,64]{2,1,0:T(8,128)S(1)}, f32[1,64,64]{2,1,0:T(8,128)}, u32[]{:S(2)}) copy-start(f32[1,64,64]{2,1,0:T(8,128)} %param.5) | copy-start | bytes 49156
  0.6 7.5 %copy-start.2 = (f32[1,64,448]{2,1,0:T(8,128)S(1)}, f32[1,64,448]{2,1,0:T(8,128)}, u32[]{:S(2)}) copy-start(f32[1,64,448]{2,1,0:T(8,128)} %param.4) | copy-start | bytes 344068
  0.7 29.4 %copy-start.1 = (f32[448,896]{1,0:T(8,128)S(1)}, f32[448,896]{1,0:T(8,128)}, u32[]{:S(2)}) copy-start(f32[448,896]{1,0:T(8,128)} %param.3) | copy-start | bytes 4816900
  4.0 15.1 %all-to-all-start = ((f32[2,32,896]{2,1,0:T(8,128)}), f32[2,32,896]{2,1,0:T(8,128)S(1)}, u32[]{:S(2)}, u32[]{:S(2)}) async-start(f32[2,32,896]{2,1,0:T(8,128)} %fusion.1), calls=%async_computation | async-start | bytes 458752 | tf_op jit(solution)/shard_map/all_to_all | solution.py:43
  8.2 0.7 collective-permute-start
  8.9 21.2 %collective-permute-start.2 = (f32[64,448]{1,0:T(8,128)S(1)}, f32[64,448]{1,0:T(8,128)S(1)}, u32[]{:S(2)}, u32[]{:S(2)}) collective-permute-start(f32[64,448]{1,0:T(8,128)S(1)} %collective-permute-done), channel_id=1, source_target_pairs={{0,0},{1,32},{2,64},{3,96},{128,128},{129,160},{130,192},{131,224}... | collective-permute-start | bytes 344072 | tf_op jit(solution)/shard_map/ppermute | solution.py:97
  15.5 14.5 %collective-permute-start.1 = (f32[64,448]{1,0:T(8,128)S(1)}, f32[64,448]{1,0:T(8,128)S(1)}, u32[]{:S(2)}, u32[]{:S(2)}) collective-permute-start(f32[64,448]{1,0:T(8,128)S(1)} %collective-permute-done), channel_id=1, source_target_pairs={{0,16},{1,48},{2,80},{3,112},{128,144},{129,176},{130,208},{131,24... | collective-permute-start | bytes 344072 | tf_op jit(solution)/shard_map/ppermute | solution.py:97
  19.8 17.9 %all-to-all-start.1 = ((f32[4,8,896]{2,1,0:T(8,128)}), f32[4,8,896]{2,1,0:T(8,128)S(1)}, u32[]{:S(2)}, u32[]{:S(2)}) async-start(f32[4,8,896]{2,1,0:T(8,128)} %bitcast.2), calls=%async_computation.1 | async-start | bytes 229376 | tf_op jit(solution)/shard_map/all_to_all | solution.py:43
  123.3 2.7 %copy-start.3 = (f32[64,448]{1,0:T(8,128)}, f32[64,448]{1,0:T(8,128)S(1)}, u32[]{:S(2)}) copy-start(f32[64,448]{1,0:T(8,128)S(1)} %fusion.4) | copy-start | bytes 344068

commit v8 on v7

--- a/solution.py
+++ b/solution.py
@@ -127,7 +127,7 @@
         mixing = contract(projected, factor, 0, 0)
         w_rows = x_rows - 0.5 * contract(mixing, v_rows, 1, 0)
         w_cols = x_cols - 0.5 * contract(mixing, v_cols, 1, 0)
-        current = current - contract(v_rows, w_cols, 0, 0) - contract(w_rows, v_cols, 0, 0)
+        current = current - contract(jnp.concatenate([v_rows, w_rows], axis=0), jnp.concatenate([w_cols, v_cols], axis=0), 0, 0)
         return (current, jnp.stack([w_rows]))
 
     return shards

time: 126 us -> 124 us (0.984)
  matrix products: 12.5 us -> 9.93 us
    dot_general x11 -> x10, matrix products: 12.5 us -> 9.93 us  [contract(): lax.dot_general(left_side, right_side, (((left_dim,), (right_dim,)), ((),...]
where the time goes in v8:
time: 124 us; the launch traced here: 123 us
  blocking collectives  80.5 us (65%)
  starting transfers between devices  25.3 us (20%)
  matrix products  9.93 us (8%)
  waiting for transfers between devices  5.96 us (5%)
    all_gather x3, blocking collectives, gathered_sum(): values = jnp.sum(lax.all_gather(values, axis), axis=0)  57.1 us
    all_gather x2, blocking collectives, scattered_sum_nested(): return lax.all_gather(mine, axes[0], tiled=True)  15.3 us
    all_to_all x2, starting transfers between devices, scattered_sum_nested(): mine = jnp.sum(lax.all_to_all(chunks, axes[0], 0, 0, tiled=False), axis=0)  14.4 us
    ppermute x2, starting transfers between devices, to_column_blocks(): lax.ppermute(moved, all_axes, [(mid, final[i]) for i, mid in first])  10.2 us
    dot_general x10, matrix products, contract(): lax.dot_general(left_side, right_side, (((left_dim,), (right_dim,)), ((),...  9.93 us
    all_gather x1, blocking collectives, split_sum(): both = lax.all_gather(total, split_axis)  8.06 us
    all_to_all x2, waiting for transfers between devices, scattered_sum_nested(): mine = jnp.sum(lax.all_to_all(chunks, axes[0], 0, 0, tiled=False), axis=0)  5.96 us
  transfers between devices with their start and end apart: 5, of which 1 were waited for; matrix products, arithmetic and copies ran while one was open for 2% of the time, Pallas kernels for 0%

profile of v8, /device:TPU:1, one launch (start us, length us, event | category | flops | bytes accessed | tf_op | source)
XLA Modules:
  0.0 123.4 jit_solution(1986075186710139976)
XLA Ops:
  0.7 3.3 %fusion = f32[2,32,896]{2,1,0:T(8,128)} fusion(f32[2,32,448]{2,1,0:T(8,128)} %bitcast.36, f32[448,896]{1,0:T(8,128)} %param.3), kind=kOutput, calls=%fused_computation | convolution fusion | flops 308281344 | bytes 1949696 | tf_op jit(solution)/shard_map/dot_general | solution.py:9
  4.0 4.2 %all-to-all-start = ((f32[2,32,896]{2,1,0:T(8,128)}), f32[2,32,896]{2,1,0:T(8,128)S(1)}, u32[]{:S(2)}, u32[]{:S(2)}) async-start(f32[2,32,896]{2,1,0:T(8,128)} %fusion), calls=%async_computation | async-start | bytes 458752 | tf_op jit(solution)/shard_map/all_to_all | solution.py:43
  8.2 0.7 collective-permute-start
  8.9 6.7 %collective-permute-start.2 = (f32[64,448]{1,0:T(8,128)S(1)}, f32[64,448]{1,0:T(8,128)S(1)}, u32[]{:S(2)}, u32[]{:S(2)}) collective-permute-start(f32[64,448]{1,0:T(8,128)S(1)} %collective-permute-done), channel_id=1, source_target_pairs={{0,0},{1,32},{2,64},{3,96},{128,128},{129,160},{130,192},{131,224}... | collective-permute-start | bytes 344072 | tf_op jit(solution)/shard_map/ppermute | solution.py:97
  15.5 3.5 %collective-permute-start.1 = (f32[64,448]{1,0:T(8,128)S(1)}, f32[64,448]{1,0:T(8,128)S(1)}, u32[]{:S(2)}, u32[]{:S(2)}) collective-permute-start(f32[64,448]{1,0:T(8,128)S(1)} %collective-permute-done), channel_id=1, source_target_pairs={{0,16},{1,48},{2,80},{3,112},{128,144},{129,176},{130,208},{131,24... | collective-permute-start | bytes 344072 | tf_op jit(solution)/shard_map/ppermute | solution.py:97
  19.1 0.7 reduce_sum.45
  19.8 10.3 %all-to-all-start.1 = ((f32[4,8,896]{2,1,0:T(8,128)}), f32[4,8,896]{2,1,0:T(8,128)S(1)}, u32[]{:S(2)}, u32[]{:S(2)}) async-start(f32[4,8,896]{2,1,0:T(8,128)} %bitcast.3), calls=%async_computation.1 | async-start | bytes 229376 | tf_op jit(solution)/shard_map/all_to_all | solution.py:43
  30.1 1.7 %fusion.14 = f32[64,448]{1,0:T(8,128)S(1)} fusion(f32[448,896]{1,0:T(8,128)S(1)} %copy-done.1, f32[64,448]{1,0:T(8,128)S(1)} %get-tuple-element.3, f32[64,448]{1,0:T(8,128)S(1)} %get-tuple-element.2), kind=kOutput, calls=%fused_computation.22 | convolution fusion | flops 308338688 | bytes 1949696 | tf_op jit(solution)/shard_map/dot_general | solution.py:9
  31.8 6.0 %all-to-all-done.1 = f32[4,8,896]{2,1,0:T(8,128)S(1)} async-done(((f32[4,8,896]{2,1,0:T(8,128)}), f32[4,8,896]{2,1,0:T(8,128)S(1)}, u32[]{:S(2)}, u32[]{:S(2)}) %all-to-all-start.1) | async-done | bytes 114720 | tf_op jit(solution)/shard_map/all_to_all | solution.py:43
  37.7 22.4 %all-gather = f32[32,896]{1,0:T(8,128)S(1)} all-gather(f32[8,896]{1,0:T(8,128)S(1)} %reduce_sum.46), channel_id=2, replica_groups=mesh['x'=4,'za'=4,'zb'=2,'y'=8,'core'=2] {'x'}, dimensions={0}, use_global_device_ids=true | all-gather | bytes 143360 | tf_op jit(solution)/shard_map/all_gather | solution.py:20
  60.1 11.0 %all_gather.32 = f32[32,896]{1,0:T(8,128)S(1)} all-gather(f32[8,896]{1,0:T(8,128)S(1)} %bitcast_reduce_fusion), channel_id=1, replica_groups=mesh['x'=4,'za'=4,'zb'=2,'y'=8,'core'=2] {'za'}, dimensions={0}, use_global_device_ids=true | all-gather | bytes 143360 | tf_op jit(solution)/shard_map/all_gather | solution.py:45
  71.1 4.3 %all_gather.33 = f32[64,896]{1,0:T(8,128)S(1)} all-gather(f32[32,896]{1,0:T(8,128)S(1)} %all_gather.32), channel_id=1, replica_groups=mesh['x'=4,'za'=4,'zb'=2,'y'=8,'core'=2] {'zb'}, dimensions={0}, use_global_device_ids=true | all-gather | bytes 344064 | tf_op jit(solution)/shard_map/all_gather | solution.py:45
  75.4 0.4 fusion.13
  75.9 0.4 convolution_bitcast_fusion
  76.3 0.1 pad_maximum_fusion.3
  76.3 11.6 %all-gather.1 = f32[128,512]{1,0:T(8,128)S(1)} all-gather(f32[64,512]{1,0:T(8,128)S(1)} %pad_maximum_fusion.3), channel_id=3, replica_groups=mesh['x'=4,'za'=4,'zb'=2,'y'=8,'core'=2] {'core'}, dimensions={0}, use_global_device_ids=true | all-gather | bytes 393216 | tf_op jit(solution)/shard_map/all_gather | solution.py:20
  88.0 23.1 %all-gather.2 = f32[512,256]{1,0:T(8,128)S(1)} all-gather(f32[64,256]{1,0:T(8,128)S(1)} %slice_select_fusion), channel_id=4, replica_groups=mesh['x'=4,'za'=4,'zb'=2,'y'=8,'core'=2] {'y'}, dimensions={0}, use_global_device_ids=true | all-gather | bytes 589824 | tf_op jit(solution)/shard_map/all_gather | solution.py:20
  111.1 8.1 %all-gather.3 = f32[128,256]{1,0:T(8,128)S(1)} all-gather(f32[64,256]{1,0:T(8,128)S(1)} %reduce_sum.49), channel_id=5, replica_groups=mesh['x'=4,'za'=4,'zb'=2,'y'=8,'core'=2] {'core'}, dimensions={0}, use_global_device_ids=true | all-gather | bytes 196608 | tf_op jit(solution)/shard_map/all_gather | solution.py:28
  119.2 0.3 fusion.15
  119.5 0.2 fusion.18
  119.8 0.3 convolution_multiply_fusion.1
  120.0 0.4 fusion.2
  120.4 0.3 fusion.3
  120.8 2.6 %convolution_subtract_fusion = f32[448,896]{1,0:T(8,128)} fusion(f32[448,896]{1,0:T(8,128)S(1)} %copy-done.1, f32[64,448]{1,0:T(8,128)S(1)} %get-tuple-element.3, f32[64,448]{1,0:T(8,128)S(1)} %get-tuple-element.2, f32[64,896]{1,0:T(8,128)S(1)} %fusion.2, f32[64,448]{1,0:T(8,128)S(1)} %fusion.3, f32[64,448]{1,0:T(8,128)S(1)} %bitcast.38), kind=kOutput, calls=%fused_computation.2 | convolution fusion | flops 617250816 | bytes 3899392 | tf_op jit(solution)/shard_map/dot_general | solution.py:9
  (19 shorter events, 0.2 us)
Async XLA Ops:
  0.6 75.2 %copy-start = (f32[1,64,64]{2,1,0:T(8,128)S(1)}, f32[1,64,64]{2,1,0:T(8,128)}, u32[]{:S(2)}) copy-start(f32[1,64,64]{2,1,0:T(8,128)} %param.5) | copy-start | bytes 49156
  0.6 7.5 %copy-start.2 = (f32[1,64,448]{2,1,0:T(8,128)S(1)}, f32[1,64,448]{2,1,0:T(8,128)}, u32[]{:S(2)}) copy-start(f32[1,64,448]{2,1,0:T(8,128)} %param.4) | copy-start | bytes 344068
  0.7 29.4 %copy-start.1 = (f32[448,896]{1,0:T(8,128)S(1)}, f32[448,896]{1,0:T(8,128)}, u32[]{:S(2)}) copy-start(f32[448,896]{1,0:T(8,128)} %param.3) | copy-start | bytes 4816900
  4.0 15.1 %all-to-all-start = ((f32[2,32,896]{2,1,0:T(8,128)}), f32[2,32,896]{2,1,0:T(8,128)S(1)}, u32[]{:S(2)}, u32[]{:S(2)}) async-start(f32[2,32,896]{2,1,0:T(8,128)} %fusion), calls=%async_computation | async-start | bytes 458752 | tf_op jit(solution)/shard_map/all_to_all | solution.py:43
  8.2 0.7 collective-permute-start
  8.9 21.2 %collective-permute-start.2 = (f32[64,448]{1,0:T(8,128)S(1)}, f32[64,448]{1,0:T(8,128)S(1)}, u32[]{:S(2)}, u32[]{:S(2)}) collective-permute-start(f32[64,448]{1,0:T(8,128)S(1)} %collective-permute-done), channel_id=1, source_target_pairs={{0,0},{1,32},{2,64},{3,96},{128,128},{129,160},{130,192},{131,224}... | collective-permute-start | bytes 344072 | tf_op jit(solution)/shard_map/ppermute | solution.py:97
  15.5 14.5 %collective-permute-start.1 = (f32[64,448]{1,0:T(8,128)S(1)}, f32[64,448]{1,0:T(8,128)S(1)}, u32[]{:S(2)}, u32[]{:S(2)}) collective-permute-start(f32[64,448]{1,0:T(8,128)S(1)} %collective-permute-done), channel_id=1, source_target_pairs={{0,16},{1,48},{2,80},{3,112},{128,144},{129,176},{130,208},{131,24... | collective-permute-start | bytes 344072 | tf_op jit(solution)/shard_map/ppermute | solution.py:97
  19.8 17.9 %all-to-all-start.1 = ((f32[4,8,896]{2,1,0:T(8,128)}), f32[4,8,896]{2,1,0:T(8,128)S(1)}, u32[]{:S(2)}, u32[]{:S(2)}) async-start(f32[4,8,896]{2,1,0:T(8,128)} %bitcast.3), calls=%async_computation.1 | async-start | bytes 229376 | tf_op jit(solution)/shard_map/all_to_all | solution.py:43
  120.8 2.7 %copy-start.3 = (f32[64,448]{1,0:T(8,128)}, f32[64,448]{1,0:T(8,128)S(1)}, u32[]{:S(2)}) copy-start(f32[64,448]{1,0:T(8,128)S(1)} %fusion.3) | copy-start | bytes 344068

commit v9 on v8

--- a/solution.py
+++ b/solution.py
@@ -113,8 +113,15 @@
         v_rows = reflectors[0]
         factor = factors[0]
         row_index = lax.axis_index(tuple(row_axes))
-        v_cols = to_column_blocks(v_rows, rows, cols, all_axes, row_index)
-        col_sums = scattered_sum_nested(contract(v_rows, current, 1, 0), row_axes[:0:-1], row_axes[:1])
+        chunks = contract(v_rows, current, 1, 0)
+        first = row_axes[-1]
+        parts = lax.axis_size(first)
+        chunks = chunks.reshape((parts, chunks.shape[0] // parts) + chunks.shape[1:])
+        mine = jnp.sum(lax.all_to_all(chunks, first, 0, 0, tiled=False), axis=0)
+        mine, v_sent = lax.optimization_barrier((mine, v_rows))
+        v_cols = to_column_blocks(v_sent, rows, cols, all_axes, row_index)
+        mine = scattered_sum_nested(mine, row_axes[-2:0:-1], row_axes[:1])
+        col_sums = lax.all_gather(mine, first, tiled=True)
         partial_value = contract(v_cols, current, 1, 1)
         partial_inner = contract(v_cols, col_sums, 1, 1)
         width = partial_value.shape[1]

time: 124 us -> 120 us (0.968)
  blocking collectives: 80.5 us -> 89.9 us
  starting transfers between devices: 25.3 us -> 18.5 us
  waiting for transfers between devices: 5.96 us -> 0.01 us
    all_to_all x0 -> x1, blocking collectives: none -> 7.84 us  [shards(): mine = jnp.sum(lax.all_to_all(chunks, first, 0, 0, tiled=False), axis=0)]
    all_to_all x2 -> x1, waiting for transfers between devices: 5.96 us -> 0.01 us  [scattered_sum_nested(): mine = jnp.sum(lax.all_to_all(chunks, axes[0], 0, 0, tiled=False), axis=0)]
    all_to_all x2 -> x1, starting transfers between devices: 14.4 us -> 9.22 us  [scattered_sum_nested(): mine = jnp.sum(lax.all_to_all(chunks, axes[0], 0, 0, tiled=False), axis=0)]
    all_gather x0 -> x1, blocking collectives: none -> 4.46 us  [shards(): col_sums = lax.all_gather(mine, first, tiled=True)]
    all_gather x2 -> x1, blocking collectives: 15.3 us -> 13.5 us  [scattered_sum_nested(): return lax.all_gather(mine, axes[0], tiled=True)]
    ppermute x2, starting transfers between devices: 10.2 us -> 8.64 us  [to_column_blocks(): lax.ppermute(moved, all_axes, [(mid, final[i]) for i, mid in first])]
  transfers between devices with their start and end apart: 5 -> 4, of which waited for: 1 -> 0; matrix products, arithmetic and copies ran while one was open for 2% -> 0% of each run, Pallas kernels for 0% -> 0%
where the time goes in v9:
time: 120 us; the launch traced here: 119 us
  blocking collectives  89.9 us (75%)
  starting transfers between devices  18.5 us (15%)
  matrix products  9.16 us (8%)
    all_gather x3, blocking collectives, gathered_sum(): values = jnp.sum(lax.all_gather(values, axis), axis=0)  56.1 us
    all_gather x1, blocking collectives, scattered_sum_nested(): return lax.all_gather(mine, axes[0], tiled=True)  13.5 us
    all_to_all x1, starting transfers between devices, scattered_sum_nested(): mine = jnp.sum(lax.all_to_all(chunks, axes[0], 0, 0, tiled=False), axis=0)  9.22 us
    dot_general x10, matrix products, contract(): lax.dot_general(left_side, right_side, (((left_dim,), (right_dim,)), ((),...  9.16 us
    ppermute x2, starting transfers between devices, to_column_blocks(): lax.ppermute(moved, all_axes, [(mid, final[i]) for i, mid in first])  8.64 us
    all_gather x1, blocking collectives, split_sum(): both = lax.all_gather(total, split_axis)  7.97 us
    all_to_all x1, blocking collectives, shards(): mine = jnp.sum(lax.all_to_all(chunks, first, 0, 0, tiled=False), axis=0)  7.84 us
    all_gather x1, blocking collectives, shards(): col_sums = lax.all_gather(mine, first, tiled=True)  4.46 us
  transfers between devices with their start and end apart: 4, of which 0 were waited for; matrix products, arithmetic and copies ran while one was open for 0% of the time, Pallas kernels for 0%

profile of v9, /device:TPU:1, one launch (start us, length us, event | category | flops | bytes accessed | tf_op | source)
XLA Modules:
  0.0 119.3 jit_solution(12330923065530089072)
XLA Ops:
  0.6 0.0 copy-start
  0.7 2.6 %fusion = f32[2,32,896]{2,1,0:T(8,128)S(1)} fusion(f32[2,32,448]{2,1,0:T(8,128)} %bitcast.36, f32[448,896]{1,0:T(8,128)} %param.3), kind=kOutput, calls=%fused_computation | convolution fusion | flops 308281344 | bytes 1949696 | tf_op jit(solution)/shard_map/dot_general | solution.py:9
  3.2 7.8 %all_to_all.10 = f32[2,32,896]{2,1,0:T(8,128)S(1)} all-to-all(f32[2,32,896]{2,1,0:T(8,128)S(1)} %fusion), channel_id=1, replica_groups=mesh['x'=4,'za'=4,'zb'=2,'y'=8,'core'=2] {'zb'}, dimensions={0} | all-to-all | bytes 458752 | tf_op jit(solution)/shard_map/all_to_all | solution.py:120
  11.1 0.7 reduce_sum.45
  11.7 9.2 %all-to-all-start.1 = ((f32[4,8,896]{2,1,0:T(8,128)}), f32[4,8,896]{2,1,0:T(8,128)S(1)}, u32[]{:S(2)}, u32[]{:S(2)}) async-start(f32[4,8,896]{2,1,0:T(8,128)} %bitcast.3), calls=%async_computation.1 | async-start | bytes 229376 | tf_op jit(solution)/shard_map/all_to_all | solution.py:43
  20.9 0.7 collective-permute-start
  21.7 6.7 %collective-permute-start.2 = (f32[64,448]{1,0:T(8,128)S(1)}, f32[64,448]{1,0:T(8,128)S(1)}, u32[]{:S(2)}, u32[]{:S(2)}) collective-permute-start(f32[64,448]{1,0:T(8,128)S(1)} %collective-permute-done), channel_id=1, source_target_pairs={{0,0},{1,32},{2,64},{3,96},{128,128},{129,160},{130,192},{131,224}... | collective-permute-start | bytes 344072 | tf_op jit(solution)/shard_map/ppermute | solution.py:97
  28.4 1.9 %collective-permute-start.1 = (f32[64,448]{1,0:T(8,128)S(1)}, f32[64,448]{1,0:T(8,128)S(1)}, u32[]{:S(2)}, u32[]{:S(2)}) collective-permute-start(f32[64,448]{1,0:T(8,128)S(1)} %collective-permute-done), channel_id=1, source_target_pairs={{0,16},{1,48},{2,80},{3,112},{128,144},{129,176},{130,208},{131,24... | collective-permute-start | bytes 344072 | tf_op jit(solution)/shard_map/ppermute | solution.py:97
  30.4 21.8 %all-gather = f32[32,896]{1,0:T(8,128)S(1)} all-gather(f32[8,896]{1,0:T(8,128)S(1)} %reduce_sum.46), channel_id=2, replica_groups=mesh['x'=4,'za'=4,'zb'=2,'y'=8,'core'=2] {'x'}, dimensions={0}, use_global_device_ids=true | all-gather | bytes 143360 | tf_op jit(solution)/shard_map/all_gather | solution.py:20
  52.2 13.5 %all_gather.32 = f32[32,896]{1,0:T(8,128)S(1)} all-gather(f32[8,896]{1,0:T(8,128)S(1)} %bitcast_reduce_fusion), channel_id=1, replica_groups=mesh['x'=4,'za'=4,'zb'=2,'y'=8,'core'=2] {'za'}, dimensions={0}, use_global_device_ids=true | all-gather | bytes 143360 | tf_op jit(solution)/shard_map/all_gather | solution.py:45
  65.7 4.5 %all_gather.33 = f32[64,896]{1,0:T(8,128)S(1)} all-gather(f32[32,896]{1,0:T(8,128)S(1)} %all_gather.32), channel_id=1, replica_groups=mesh['x'=4,'za'=4,'zb'=2,'y'=8,'core'=2] {'zb'}, dimensions={0}, use_global_device_ids=true | all-gather | bytes 344064 | tf_op jit(solution)/shard_map/all_gather | solution.py:124
  70.2 0.4 convolution_bitcast_fusion
  70.6 0.4 fusion.13
  71.0 1.7 %fusion.14 = f32[64,448]{1,0:T(8,128)S(1)} fusion(f32[448,896]{1,0:T(8,128)S(1)} %copy-done.1, f32[64,448]{1,0:T(8,128)S(1)} %get-tuple-element.7, f32[64,448]{1,0:T(8,128)S(1)} %get-tuple-element.6), kind=kOutput, calls=%fused_computation.22 | convolution fusion | flops 308338688 | bytes 1949696 | tf_op jit(solution)/shard_map/dot_general | solution.py:9
  72.7 0.1 pad_maximum_fusion.3
  72.8 11.5 %all-gather.1 = f32[128,512]{1,0:T(8,128)S(1)} all-gather(f32[64,512]{1,0:T(8,128)S(1)} %pad_maximum_fusion.3), channel_id=3, replica_groups=mesh['x'=4,'za'=4,'zb'=2,'y'=8,'core'=2] {'core'}, dimensions={0}, use_global_device_ids=true | all-gather | bytes 393216 | tf_op jit(solution)/shard_map/all_gather | solution.py:20
  84.3 22.8 %all-gather.2 = f32[512,256]{1,0:T(8,128)S(1)} all-gather(f32[64,256]{1,0:T(8,128)S(1)} %slice_select_fusion), channel_id=4, replica_groups=mesh['x'=4,'za'=4,'zb'=2,'y'=8,'core'=2] {'y'}, dimensions={0}, use_global_device_ids=true | all-gather | bytes 589824 | tf_op jit(solution)/shard_map/all_gather | solution.py:20
  107.1 8.0 %all-gather.3 = f32[128,256]{1,0:T(8,128)S(1)} all-gather(f32[64,256]{1,0:T(8,128)S(1)} %reduce_sum.49), channel_id=5, replica_groups=mesh['x'=4,'za'=4,'zb'=2,'y'=8,'core'=2] {'core'}, dimensions={0}, use_global_device_ids=true | all-gather | bytes 196608 | tf_op jit(solution)/shard_map/all_gather | solution.py:28
  115.1 0.3 fusion.15
  115.4 0.2 fusion.18
  115.7 0.3 convolution_multiply_fusion.1
  115.9 0.4 fusion.2
  116.3 0.3 fusion.3
  116.7 2.6 %convolution_subtract_fusion = f32[448,896]{1,0:T(8,128)} fusion(f32[448,896]{1,0:T(8,128)S(1)} %copy-done.1, f32[64,448]{1,0:T(8,128)S(1)} %get-tuple-element.7, f32[64,448]{1,0:T(8,128)S(1)} %get-tuple-element.6, f32[64,896]{1,0:T(8,128)S(1)} %fusion.2, f32[64,448]{1,0:T(8,128)S(1)} %fusion.3, f32[64,448]{1,0:T(8,128)S(1)} %bitcast.38), kind=kOutput, calls=%fused_computation.2 | convolution fusion | flops 617250816 | bytes 3899392 | tf_op jit(solution)/shard_map/dot_general | solution.py:9
  (18 shorter events, 0.1 us)
Async XLA Ops:
  0.6 69.5 %copy-start = (f32[1,64,64]{2,1,0:T(8,128)S(1)}, f32[1,64,64]{2,1,0:T(8,128)}, u32[]{:S(2)}) copy-start(f32[1,64,64]{2,1,0:T(8,128)} %param.5) | copy-start | bytes 49156
  0.6 20.3 %copy-start.2 = (f32[1,64,448]{2,1,0:T(8,128)S(1)}, f32[1,64,448]{2,1,0:T(8,128)}, u32[]{:S(2)}) copy-start(f32[1,64,448]{2,1,0:T(8,128)} %param.4) | copy-start | bytes 344068
  11.1 60.0 %copy-start.1 = (f32[448,896]{1,0:T(8,128)S(1)}, f32[448,896]{1,0:T(8,128)}, u32[]{:S(2)}) copy-start(f32[448,896]{1,0:T(8,128)} %param.3) | copy-start | bytes 4816900
  11.7 18.6 %all-to-all-start.1 = ((f32[4,8,896]{2,1,0:T(8,128)}), f32[4,8,896]{2,1,0:T(8,128)S(1)}, u32[]{:S(2)}, u32[]{:S(2)}) async-start(f32[4,8,896]{2,1,0:T(8,128)} %bitcast.3), calls=%async_computation.1 | async-start | bytes 229376 | tf_op jit(solution)/shard_map/all_to_all | solution.py:43
  20.9 0.7 collective-permute-start
  21.7 48.9 %collective-permute-start.2 = (f32[64,448]{1,0:T(8,128)S(1)}, f32[64,448]{1,0:T(8,128)S(1)}, u32[]{:S(2)}, u32[]{:S(2)}) collective-permute-start(f32[64,448]{1,0:T(8,128)S(1)} %collective-permute-done), channel_id=1, source_target_pairs={{0,0},{1,32},{2,64},{3,96},{128,128},{129,160},{130,192},{131,224}... | collective-permute-start | bytes 344072 | tf_op jit(solution)/shard_map/ppermute | solution.py:97
  28.4 42.2 %collective-permute-start.1 = (f32[64,448]{1,0:T(8,128)S(1)}, f32[64,448]{1,0:T(8,128)S(1)}, u32[]{:S(2)}, u32[]{:S(2)}) collective-permute-start(f32[64,448]{1,0:T(8,128)S(1)} %collective-permute-done), channel_id=1, source_target_pairs={{0,16},{1,48},{2,80},{3,112},{128,144},{129,176},{130,208},{131,24... | collective-permute-start | bytes 344072 | tf_op jit(solution)/shard_map/ppermute | solution.py:97
  116.7 2.7 %copy-start.3 = (f32[64,448]{1,0:T(8,128)}, f32[64,448]{1,0:T(8,128)S(1)}, u32[]{:S(2)}) copy-start(f32[64,448]{1,0:T(8,128)S(1)} %fusion.3) | copy-start | bytes 344068

commit v10 on v9

--- a/solution.py
+++ b/solution.py
@@ -105,6 +105,23 @@
     return jnp.concatenate(blocks, axis=values.ndim - 1)
 
 
+def second_hops(moved, rows, cols, all_axes, row_index):
+    group = rows // cols
+    first = staged_route(rows, cols)
+    rounds = []
+    for shift in range(group):
+        final = dict(column_block_pairs(rows, cols, shift))
+        rounds.append(lax.ppermute(moved, all_axes, [(mid, final[i]) for i, mid in first]))
+    offset = row_index % group
+    blocks = []
+    for part in range(group):
+        block = rounds[0]
+        for shift in range(1, group):
+            block = jnp.where((part - offset) % group == shift, rounds[shift], block)
+        blocks.append(block)
+    return jnp.concatenate(blocks, axis=moved.ndim - 1)
+
+
 def make_shards(row_axes, col_axes, rows, cols):
     all_axes = tuple(row_axes) + tuple(col_axes)
 
@@ -119,8 +136,15 @@
         chunks = chunks.reshape((parts, chunks.shape[0] // parts) + chunks.shape[1:])
         mine = jnp.sum(lax.all_to_all(chunks, first, 0, 0, tiled=False), axis=0)
         mine, v_sent = lax.optimization_barrier((mine, v_rows))
-        v_cols = to_column_blocks(v_sent, rows, cols, all_axes, row_index)
-        mine = scattered_sum_nested(mine, row_axes[-2:0:-1], row_axes[:1])
+        moved = lax.ppermute(v_sent, all_axes, staged_route(rows, cols))
+        second = row_axes[-2]
+        parts2 = lax.axis_size(second)
+        chunks = mine.reshape((parts2, mine.shape[0] // parts2) + mine.shape[1:])
+        mine = jnp.sum(lax.all_to_all(chunks, second, 0, 0, tiled=False), axis=0)
+        mine = gathered_sum(mine, row_axes[:1])
+        mine, moved = lax.optimization_barrier((mine, moved))
+        v_cols = second_hops(moved, rows, cols, all_axes, row_index)
+        mine = lax.all_gather(mine, second, tiled=True)
         col_sums = lax.all_gather(mine, first, tiled=True)
         partial_value = contract(v_cols, current, 1, 1)
         partial_inner = contract(v_cols, col_sums, 1, 1)

time: 120 us -> 112 us (0.933)
  blocking collectives: 89.9 us -> 72.6 us
  waiting for transfers between devices: 0.01 us -> 6.48 us
  starting transfers between devices: 18.5 us -> 21.4 us
    all_gather x3, blocking collectives: 56.1 us -> 35.6 us  [gathered_sum(): values = jnp.sum(lax.all_gather(values, axis), axis=0)]
    all_to_all x1, waiting for transfers between devices: 0.01 us -> 6.47 us  [shards(): mine = jnp.sum(lax.all_to_all(chunks, second, 0, 0, tiled=False), axis=0)]
    all_gather x1, blocking collectives: 13.5 us -> 17 us  [shards(): mine = lax.all_gather(mine, second, tiled=True)]
    ppermute x3, starting transfers between devices: 9.29 us -> 12.1 us  [the longest x2 11.5 us: second_hops(): lax.ppermute(moved, all_axes, [(mid, final[i]) for i, mid in first])]
  transfers between devices with their start and end apart: 4 -> 4, of which waited for: 0 -> 1; matrix products, arithmetic and copies ran while one was open for 0% -> 0% of each run, Pallas kernels for 0% -> 0%
where the time goes in v10:
time: 112 us; the launch traced here: 111 us
  blocking collectives  72.6 us (65%)
  starting transfers between devices  21.4 us (19%)
  matrix products  9.15 us (8%)
  waiting for transfers between devices  6.48 us (6%)
    all_gather x3, blocking collectives, gathered_sum(): values = jnp.sum(lax.all_gather(values, axis), axis=0)  35.6 us
    all_gather x1, blocking collectives, shards(): mine = lax.all_gather(mine, second, tiled=True)  17 us
    ppermute x2, starting transfers between devices, second_hops(): lax.ppermute(moved, all_axes, [(mid, final[i]) for i, mid in first])  11.5 us
    all_to_all x1, starting transfers between devices, shards(): mine = jnp.sum(lax.all_to_all(chunks, second, 0, 0, tiled=False), axis=0)  9.22 us
    dot_general x10, matrix products, contract(): lax.dot_general(left_side, right_side, (((left_dim,), (right_dim,)), ((),...  9.15 us
    all_gather x1, blocking collectives, split_sum(): both = lax.all_gather(total, split_axis)  7.91 us
    all_to_all x1, blocking collectives, shards(): mine = jnp.sum(lax.all_to_all(chunks, first, 0, 0, tiled=False), axis=0)  7.84 us
    all_to_all x1, waiting for transfers between devices, shards(): mine = jnp.sum(lax.all_to_all(chunks, second, 0, 0, tiled=False), axis=0)  6.47 us
  transfers between devices with their start and end apart: 4, of which 1 were waited for; matrix products, arithmetic and copies ran while one was open for 0% of the time, Pallas kernels for 0%

profile of v10, /device:TPU:1, one launch (start us, length us, event | category | flops | bytes accessed | tf_op | source)
XLA Modules:
  0.0 111.3 jit_solution(5235569078798116109)
XLA Ops:
  0.7 2.6 %fusion = f32[2,32,896]{2,1,0:T(8,128)S(1)} fusion(f32[2,32,448]{2,1,0:T(8,128)} %bitcast.36, f32[448,896]{1,0:T(8,128)} %param.3), kind=kOutput, calls=%fused_computation | convolution fusion | flops 308281344 | bytes 1949696 | tf_op jit(solution)/shard_map/dot_general | solution.py:9
  3.2 7.8 %all_to_all.10 = f32[2,32,896]{2,1,0:T(8,128)S(1)} all-to-all(f32[2,32,896]{2,1,0:T(8,128)S(1)} %fusion), channel_id=1, replica_groups=mesh['x'=4,'za'=4,'zb'=2,'y'=8,'core'=2] {'zb'}, dimensions={0} | all-to-all | bytes 458752 | tf_op jit(solution)/shard_map/all_to_all | solution.py:137
  11.1 0.7 reduce_sum.45
  11.7 9.2 %all-to-all-start.1 = ((f32[4,8,896]{2,1,0:T(8,128)}), f32[4,8,896]{2,1,0:T(8,128)S(1)}, u32[]{:S(2)}, u32[]{:S(2)}) async-start(f32[4,8,896]{2,1,0:T(8,128)} %bitcast.3), calls=%async_computation.1 | async-start | bytes 229376 | tf_op jit(solution)/shard_map/all_to_all | solution.py:143
  20.9 0.7 collective-permute-start
  21.6 6.5 %all-to-all-done.1 = f32[4,8,896]{2,1,0:T(8,128)S(1)} async-done(((f32[4,8,896]{2,1,0:T(8,128)}), f32[4,8,896]{2,1,0:T(8,128)S(1)}, u32[]{:S(2)}, u32[]{:S(2)}) %all-to-all-start.1) | async-done | bytes 114720 | tf_op jit(solution)/shard_map/all_to_all | solution.py:143
  28.1 10.1 %all-gather = f32[32,896]{1,0:T(8,128)S(1)} all-gather(f32[8,896]{1,0:T(8,128)S(1)} %reduce_sum.46), channel_id=2, replica_groups=mesh['x'=4,'za'=4,'zb'=2,'y'=8,'core'=2] {'x'}, dimensions={0}, use_global_device_ids=true | all-gather | bytes 143360 | tf_op jit(solution)/shard_map/all_gather | solution.py:20
  38.2 9.6 %collective-permute-start.2 = (f32[64,448]{1,0:T(8,128)S(1)}, f32[64,448]{1,0:T(8,128)S(1)}, u32[]{:S(2)}, u32[]{:S(2)}) collective-permute-start(f32[64,448]{1,0:T(8,128)S(1)} %collective-permute-done), channel_id=1, source_target_pairs={{0,0},{1,32},{2,64},{3,96},{128,128},{129,160},{130,192},{131,224}... | collective-permute-start | bytes 344072 | tf_op jit(solution)/shard_map/ppermute | solution.py:114
  47.8 1.9 %collective-permute-start.1 = (f32[64,448]{1,0:T(8,128)S(1)}, f32[64,448]{1,0:T(8,128)S(1)}, u32[]{:S(2)}, u32[]{:S(2)}) collective-permute-start(f32[64,448]{1,0:T(8,128)S(1)} %collective-permute-done), channel_id=1, source_target_pairs={{0,16},{1,48},{2,80},{3,112},{128,144},{129,176},{130,208},{131,24... | collective-permute-start | bytes 344072 | tf_op jit(solution)/shard_map/ppermute | solution.py:114
  49.7 17.0 %all_gather.32 = f32[32,896]{1,0:T(8,128)S(1)} all-gather(f32[8,896]{1,0:T(8,128)S(1)} %bitcast_reduce_fusion), channel_id=1, replica_groups=mesh['x'=4,'za'=4,'zb'=2,'y'=8,'core'=2] {'za'}, dimensions={0}, use_global_device_ids=true | all-gather | bytes 143360 | tf_op jit(solution)/shard_map/all_gather | solution.py:147
  66.8 4.3 %all_gather.33 = f32[64,896]{1,0:T(8,128)S(1)} all-gather(f32[32,896]{1,0:T(8,128)S(1)} %all_gather.32), channel_id=1, replica_groups=mesh['x'=4,'za'=4,'zb'=2,'y'=8,'core'=2] {'zb'}, dimensions={0}, use_global_device_ids=true | all-gather | bytes 344064 | tf_op jit(solution)/shard_map/all_gather | solution.py:148
  71.1 0.4 convolution_bitcast_fusion
  71.5 0.4 fusion.13
  71.9 1.7 %fusion.14 = f32[64,448]{1,0:T(8,128)S(1)} fusion(f32[448,896]{1,0:T(8,128)S(1)} %copy-done.1, f32[64,448]{1,0:T(8,128)S(1)} %get-tuple-element.11, f32[64,448]{1,0:T(8,128)S(1)} %get-tuple-element.10), kind=kOutput, calls=%fused_computation.22 | convolution fusion | flops 308338688 | bytes 1949696 | tf_op jit(solution)/shard_map/dot_general | solution.py:9
  73.6 0.1 pad_maximum_fusion.3
  73.7 5.9 %all-gather.1 = f32[128,512]{1,0:T(8,128)S(1)} all-gather(f32[64,512]{1,0:T(8,128)S(1)} %pad_maximum_fusion.3), channel_id=3, replica_groups=mesh['x'=4,'za'=4,'zb'=2,'y'=8,'core'=2] {'core'}, dimensions={0}, use_global_device_ids=true | all-gather | bytes 393216 | tf_op jit(solution)/shard_map/all_gather | solution.py:20
  79.6 19.5 %all-gather.2 = f32[512,256]{1,0:T(8,128)S(1)} all-gather(f32[64,256]{1,0:T(8,128)S(1)} %slice_select_fusion), channel_id=4, replica_groups=mesh['x'=4,'za'=4,'zb'=2,'y'=8,'core'=2] {'y'}, dimensions={0}, use_global_device_ids=true | all-gather | bytes 589824 | tf_op jit(solution)/shard_map/all_gather | solution.py:20
  99.2 7.9 %all-gather.3 = f32[128,256]{1,0:T(8,128)S(1)} all-gather(f32[64,256]{1,0:T(8,128)S(1)} %reduce_sum.49), channel_id=5, replica_groups=mesh['x'=4,'za'=4,'zb'=2,'y'=8,'core'=2] {'core'}, dimensions={0}, use_global_device_ids=true | all-gather | bytes 196608 | tf_op jit(solution)/shard_map/all_gather | solution.py:28
  107.1 0.3 fusion.15
  107.4 0.2 fusion.18
  107.7 0.3 convolution_multiply_fusion.1
  107.9 0.4 fusion.2
  108.3 0.3 fusion.3
  108.7 2.6 %convolution_subtract_fusion = f32[448,896]{1,0:T(8,128)} fusion(f32[448,896]{1,0:T(8,128)S(1)} %copy-done.1, f32[64,448]{1,0:T(8,128)S(1)} %get-tuple-element.11, f32[64,448]{1,0:T(8,128)S(1)} %get-tuple-element.10, f32[64,896]{1,0:T(8,128)S(1)} %fusion.2, f32[64,448]{1,0:T(8,128)S(1)} %fusion.3, f32[64,448]{1,0:T(8,128)S(1)} %bitcast.38), kind=kOutput, calls=%fused_computation.2 | convolution fusion | flops 617250816 | bytes 3899392 | tf_op jit(solution)/shard_map/dot_general | solution.py:9
  (18 shorter events, 0.1 us)
Async XLA Ops:
  0.6 70.4 %copy-start = (f32[1,64,64]{2,1,0:T(8,128)S(1)}, f32[1,64,64]{2,1,0:T(8,128)}, u32[]{:S(2)}) copy-start(f32[1,64,64]{2,1,0:T(8,128)} %param.5) | copy-start | bytes 49156
  0.6 20.3 %copy-start.2 = (f32[1,64,448]{2,1,0:T(8,128)S(1)}, f32[1,64,448]{2,1,0:T(8,128)}, u32[]{:S(2)}) copy-start(f32[1,64,448]{2,1,0:T(8,128)} %param.4) | copy-start | bytes 344068
  11.1 60.9 %copy-start.1 = (f32[448,896]{1,0:T(8,128)S(1)}, f32[448,896]{1,0:T(8,128)}, u32[]{:S(2)}) copy-start(f32[448,896]{1,0:T(8,128)} %param.3) | copy-start | bytes 4816900
  11.7 16.4 %all-to-all-start.1 = ((f32[4,8,896]{2,1,0:T(8,128)}), f32[4,8,896]{2,1,0:T(8,128)S(1)}, u32[]{:S(2)}, u32[]{:S(2)}) async-start(f32[4,8,896]{2,1,0:T(8,128)} %bitcast.3), calls=%async_computation.1 | async-start | bytes 229376 | tf_op jit(solution)/shard_map/all_to_all | solution.py:143
  20.9 17.3 %collective-permute-start = (f32[64,448]{1,0:T(8,128)S(1)}, f32[64,448]{1,0:T(8,128)S(1)}, u32[]{:S(2)}, u32[]{:S(2)}) collective-permute-start(f32[64,448]{1,0:T(8,128)S(1)} %bitcast.37), channel_id=1, source_target_pairs={{0,0},{1,1},{2,2},{3,3},{4,128},{5,129},{6,130},{7,131},{8,256},{9... | collective-permute-start | bytes 344072 | tf_op jit(solution)/shard_map/ppermute | solution.py:139
  38.2 33.2 %collective-permute-start.2 = (f32[64,448]{1,0:T(8,128)S(1)}, f32[64,448]{1,0:T(8,128)S(1)}, u32[]{:S(2)}, u32[]{:S(2)}) collective-permute-start(f32[64,448]{1,0:T(8,128)S(1)} %collective-permute-done), channel_id=1, source_target_pairs={{0,0},{1,32},{2,64},{3,96},{128,128},{129,160},{130,192},{131,224}... | collective-permute-start | bytes 344072 | tf_op jit(solution)/shard_map/ppermute | solution.py:114
  47.8 23.7 %collective-permute-start.1 = (f32[64,448]{1,0:T(8,128)S(1)}, f32[64,448]{1,0:T(8,128)S(1)}, u32[]{:S(2)}, u32[]{:S(2)}) collective-permute-start(f32[64,448]{1,0:T(8,128)S(1)} %collective-permute-done), channel_id=1, source_target_pairs={{0,16},{1,48},{2,80},{3,112},{128,144},{129,176},{130,208},{131,24... | collective-permute-start | bytes 344072 | tf_op jit(solution)/shard_map/ppermute | solution.py:114
  108.7 2.7 %copy-start.3 = (f32[64,448]{1,0:T(8,128)}, f32[64,448]{1,0:T(8,128)S(1)}, u32[]{:S(2)}) copy-start(f32[64,448]{1,0:T(8,128)S(1)} %fusion.3) | copy-start | bytes 344068
